TPU v7x, 32 devices: a whole 2x2x4 slice. The times are simulated.
32 devices in a mesh: groups: 2 (over y), ctx: 4 (over x, core), dp: 4 (over z).
Axes of the slice: x: 2, y: 2, z: 4, core: 2. Of those that a mesh axis runs over, the one named last changes fastest.
Arguments:
- hidden_in: bfloat16 [8192, 1536], P(('groups', 'ctx', 'dp')), parts along dimension 0, may hold values from -0.119628906 to 0.119628906
- queries: bfloat16 [8192, 1536], P(('groups', 'ctx', 'dp')), parts along dimension 0, may hold values from -60 to 60
- keys: bfloat16 [8192, 256], P(('groups', 'ctx', 'dp')), parts along dimension 0, may hold values from -60 to 60
- values: bfloat16 [8192, 256], P(('groups', 'ctx', 'dp')), parts along dimension 0, may hold values from -6 to 6
- out_grad: bfloat16 [8192, 1536], P(('groups', 'ctx', 'dp')), parts along dimension 0, may hold values from -48 to 48
- segment_ids: int32 [8192], P('groups'), parts along dimension 0, may hold values from 0 to 15, never falling along the last dimension, each value on 1 to 512 neighbouring positions
Outputs:
- query_grad: bfloat16 [8192, 1536], P(('groups', 'ctx', 'dp')), parts along dimension 0
- kv_weight_grad: float32 [3072, 512], P(('groups', 'dp')), parts along dimension 0
There are 2 independent parts, one for each index of `groups`. A program takes and returns all parts, laid end to end along the dimension named above; each array names one. Nothing has to cross between parts.
Inputs may be any that keep to these rules, and one draw needn't show every extreme that they name: `segment_ids`: the ids never fall along the tokens; each rollout takes 1 to 512 consecutive positions, and one takes exactly 512.
All inputs are finite; a program needn't handle non-finite values.
Results may differ from a plain program's by a relative error of at most 0.0049.
Values may be sent and summed in bfloat16 or wider, within the bound.
No kernel may reach another device: no remote copies, remote signals or barrier semaphores. Data moves between devices by JAX's collectives and lax.ppermute only.
A program may use at most 64 MiB of HBM per device.

v0:
```python
import jax
import jax.numpy as jnp
from jax import lax
from jax.sharding import PartitionSpec as P

QUERY_HEADS = 12
KEY_VALUE_HEADS = 2
HEAD_SIZE = 128


def shifted(block, axis, distance):
    devices = range(lax.axis_size(axis))
    route = [(i - distance, i) for i in devices if i - distance in devices]
    return lax.ppermute(block, axis, route)


def window_grads(block_of_query, key_span_window, value_span_window, block_gradient, visible):
    rows_per_block = block_of_query.shape[0]
    rows_in_span = key_span_window.shape[0]
    group_width = QUERY_HEADS // KEY_VALUE_HEADS
    scale = HEAD_SIZE ** (-0.5)
    heads_of_query = block_of_query.reshape(rows_per_block, KEY_VALUE_HEADS, group_width, HEAD_SIZE)
    head_gradients = block_gradient.reshape(rows_per_block, KEY_VALUE_HEADS, group_width, HEAD_SIZE)
    heads_of_key = key_span_window.reshape(rows_in_span, KEY_VALUE_HEADS, HEAD_SIZE)
    heads_of_value = value_span_window.reshape(rows_in_span, KEY_VALUE_HEADS, HEAD_SIZE)
    query_parts = []
    key_pieces = []
    value_pieces = []
    for head_position in range(KEY_VALUE_HEADS):
        query_now = heads_of_query[:, head_position]
        grad_now = head_gradients[:, head_position]
        key_now = heads_of_key[:, head_position]
        value_now = heads_of_value[:, head_position]
        scores = (
            jnp.einsum("tgd,sd->gts", query_now, key_now, preferred_element_type=jnp.float32)
            * scale
        )
        scores = jnp.where(visible[None], scores, -jnp.inf)
        top = jnp.max(scores, axis=-1, keepdims=True)
        expo = jnp.exp(scores - top)
        probs = expo / jnp.sum(expo, axis=-1, keepdims=True)
        probs_low = probs.astype(jnp.bfloat16)
        dprobs = jnp.einsum("tgd,sd->gts", grad_now, value_now, preferred_element_type=jnp.float32)
        delta = jnp.sum(probs * dprobs, axis=-1, keepdims=True)
        dscores_low = (probs * (dprobs - delta)).astype(jnp.bfloat16)
        value_pieces.append(
            jnp.einsum("gts,tgd->sd", probs_low, grad_now, preferred_element_type=jnp.float32)
        )
        key_pieces.append(
            jnp.einsum("gts,tgd->sd", dscores_low, query_now, preferred_element_type=jnp.float32)
            * scale
        )
        query_parts.append(
            jnp.einsum("gts,sd->tgd", dscores_low, key_now, preferred_element_type=jnp.float32)
            * scale
        )
    query_grad = jnp.stack(query_parts, 1).reshape(rows_per_block, QUERY_HEADS * HEAD_SIZE)
    key_gradient = jnp.stack(key_pieces, 1).reshape(rows_in_span, KEY_VALUE_HEADS * HEAD_SIZE)
    value_gradient = jnp.stack(value_pieces, 1).reshape(rows_in_span, KEY_VALUE_HEADS * HEAD_SIZE)
    return (query_grad, jnp.concatenate([key_gradient, value_gradient], 1))


def weight_term(hidden_block, kv_grad):
    return jnp.einsum(
        "td,tc->dc", hidden_block.astype(jnp.float32), kv_grad, precision=lax.Precision.HIGHEST
    )


def on_device(hidden_in, queries, keys, values, out_grad, segment_ids):
    rows_per_block = queries.shape[0]
    cycle_place = lax.axis_index(("ctx", "dp"))
    prev_keys, prev_values = shifted((keys, values), ("ctx", "dp"), 1)
    key_span_window = jnp.concatenate([prev_keys, keys], 0)
    value_span_window = jnp.concatenate([prev_values, values], 0)
    own_segments = lax.dynamic_slice_in_dim(
        segment_ids, cycle_place * rows_per_block, rows_per_block, 0
    )
    prev_segments = lax.dynamic_slice_in_dim(
        segment_ids, jnp.maximum(cycle_place - 1, 0) * rows_per_block, rows_per_block, 0
    )
    key_segments = jnp.concatenate([prev_segments, own_segments], 0)
    query_rows = jnp.arange(rows_per_block, dtype=jnp.int32)[:, None]
    key_cols = jnp.arange(2 * rows_per_block, dtype=jnp.int32)[None, :]
    visible = (key_cols <= query_rows + rows_per_block) & (
        (key_cols >= rows_per_block) | (cycle_place > 0)
    )
    visible = visible & (key_segments[None, :] == own_segments[:, None])
    query_grad, kv_window = window_grads(
        queries, key_span_window, value_span_window, out_grad, visible
    )
    returned = shifted(kv_window[:rows_per_block].astype(jnp.bfloat16), ("ctx", "dp"), -1).astype(
        jnp.float32
    )
    term = weight_term(hidden_in, kv_window[rows_per_block:] + returned)
    total_rows = term.shape[0]
    replica_count = lax.axis_size("dp")
    whole = lax.psum(term, ("ctx", "dp"))
    share = total_rows // replica_count
    weight_grad = lax.dynamic_slice_in_dim(whole, lax.axis_index("dp") * share, share, 0)
    return (query_grad.astype(jnp.bfloat16), weight_grad)


def solution(mesh):
    return jax.shard_map(
        on_device,
        mesh=mesh,
        in_specs=(
            P(("groups", "ctx", "dp"), None),
            P(("groups", "ctx", "dp"), None),
            P(("groups", "ctx", "dp"), None),
            P(("groups", "ctx", "dp"), None),
            P(("groups", "ctx", "dp"), None),
            P("groups"),
        ),
        out_specs=(P(("groups", "ctx", "dp"), None), P(("groups", "dp"), None)),
        check_vma=False,
    )
```

profile of v0, /device:TPU:0, one launch (start us, length us, event | category | flops | bytes accessed | tf_op | source)
XLA Modules:
  0.0 159.0 jit_solution(12490290141752014390)
XLA Ops:
  7.2 1.1 copy.27
  8.3 4.9 %collective-permute-start.1 = (bf16[256,256]{0,1:T(8,128)(2,1)S(1)}, bf16[256,256]{0,1:T(8,128)(2,1)S(1)}, u32[]{:S(2)}, u32[]{:S(2)}) collective-permute-start(bf16[256,256]{0,1:T(8,128)(2,1)S(1)} %copy.27), channel_id=1, source_target_pairs={{0,1},{1,2},{2,3},{3,4},{4,5},{5,6},{6,7},{7,8},{8,9},{9,10},{10,1... | collective-permute-start | bytes 393224 | tf_op jit(solution)/shard_map/ppermute | solution.py:14
  13.2 1.0 copy.22
  14.3 3.5 %collective-permute-start = (bf16[256,256]{0,1:T(8,128)(2,1)S(1)}, bf16[256,256]{0,1:T(8,128)(2,1)S(1)}, u32[]{:S(2)}, u32[]{:S(2)}) collective-permute-start(bf16[256,256]{0,1:T(8,128)(2,1)S(1)} %copy.22), channel_id=1, source_target_pairs={{0,1},{1,2},{2,3},{3,4},{4,5},{5,6},{6,7},{7,8},{8,9},{9,10},{10,1... | collective-permute-start | bytes 393224 | tf_op jit(solution)/shard_map/ppermute | solution.py:14
  17.8 1.4 copy.25
  19.2 1.4 copy.30
  20.6 0.8 fusion.51
  22.9 1.4 fusion.52
  24.3 0.6 fusion.27
  25.0 1.5 fusion.53
  26.5 0.6 fusion.2
  27.1 0.6 fusion.24
  27.8 0.6 fusion.5
  28.9 0.6 fusion.31
  30.0 1.1 copy-done.1
  31.1 0.6 fusion.33
  31.9 1.3 collective-permute-start.2
  33.2 9.2 %collective-permute-done.2 = bf16[256,512]{0,1:T(8,128)(2,1)S(1)} collective-permute-done((bf16[256,512]{0,1:T(8,128)(2,1)S(1)}, bf16[256,512]{0,1:T(8,128)(2,1)S(1)}, u32[]{:S(2)}, u32[]{:S(2)}) %collective-permute-start.2) | collective-permute-done | bytes 262176 | tf_op jit(solution)/shard_map/ppermute | solution.py:14
  42.4 3.1 %convolution_bitcast_fusion = f32[1536,512]{0,1:T(8,128)} fusion(bf16[256,1536]{1,0:T(8,128)(2,1)S(1)} %copy-done, f32[512,256]{0,1:T(8,128)S(1)} %bitcast.147, f32[512,256]{0,1:T(8,128)S(1)} %bitcast.145, bf16[256,512]{0,1:T(8,128)(2,1)S(1)} %collective-permute-done.2), kind=kOutput, calls=%fused_computation.2 | convolution fusion | flops 2416312320 | bytes 5242880 | tf_op jit(solution)/shard_map/td,tc->dc/dot_general | solution.py:64
  45.9 1.8 %fusion.23 = bf16[256,1,6,128]{0,3,2,1:T(8,128)(2,1)S(1)} fusion(bf16[6,256,512]{1,2,0:T(8,128)(2,1)} %copy-done.1, bf16[512,2,128]{0,2,1:T(8,128)(2,1)S(1)} %bitcast.156), kind=kOutput, calls=%fused_computation.36 | convolution fusion | flops 201719808 | bytes 2097152 | tf_op jit(solution)/shard_map/gts,sd->tgd/dot_general | solution.py:54
  47.8 1.2 copy.48
  48.9 100.9 %all-reduce.2.cloned.1.call-done = f32[1536,512]{0,1:T(8,128)} async-done(((f32[1536,512]{0,1:T(8,128)}), f32[1536,512]{0,1:T(8,128)}) %all-reduce.2.cloned.1.call-update) | async-done | bytes 3145744 | tf_op jit(solution)/shard_map/psum | solution.py:97
  149.9 1.2 constant_dynamic-slice_fusion
  151.0 1.1 copy.49
  (22 shorter events, 3.0 us)
Async XLA Ops:
  7.2 35.2 %copy-start = (bf16[256,1536]{1,0:T(8,128)(2,1)S(1)}, bf16[256,1536]{1,0:T(8,128)(2,1)}, u32[]{:S(2)}) copy-start(bf16[256,1536]{1,0:T(8,128)(2,1)} %param.6) | copy-start | bytes 2359300
  7.2 142.7 %all-reduce.2.cloned.1.call-start = ((), (), s32[]{:S(2)}) async-start(), calls=%async_computation | async-start | bytes 6291456 | tf_op jit(solution)/shard_map/psum | solution.py:97
  8.3 18.2 %collective-permute-start.1 = (bf16[256,256]{0,1:T(8,128)(2,1)S(1)}, bf16[256,256]{0,1:T(8,128)(2,1)S(1)}, u32[]{:S(2)}, u32[]{:S(2)}) collective-permute-start(bf16[256,256]{0,1:T(8,128)(2,1)S(1)} %copy.27), channel_id=1, source_target_pairs={{0,1},{1,2},{2,3},{3,4},{4,5},{5,6},{6,7},{7,8},{8,9},{9,10},{10,1... | collective-permute-start | bytes 393224 | tf_op jit(solution)/shard_map/ppermute | solution.py:14
  14.3 7.4 %collective-permute-start = (bf16[256,256]{0,1:T(8,128)(2,1)S(1)}, bf16[256,256]{0,1:T(8,128)(2,1)S(1)}, u32[]{:S(2)}, u32[]{:S(2)}) collective-permute-start(bf16[256,256]{0,1:T(8,128)(2,1)S(1)} %copy.22), channel_id=1, source_target_pairs={{0,1},{1,2},{2,3},{3,4},{4,5},{5,6},{6,7},{7,8},{8,9},{9,10},{10,1... | collective-permute-start | bytes 393224 | tf_op jit(solution)/shard_map/ppermute | solution.py:14
  30.0 1.1 copy-start.1
  31.9 10.5 %collective-permute-start.2 = (bf16[256,512]{0,1:T(8,128)(2,1)S(1)}, bf16[256,512]{0,1:T(8,128)(2,1)S(1)}, u32[]{:S(2)}, u32[]{:S(2)}) collective-permute-start(bf16[256,512]{0,1:T(8,128)(2,1)S(1)} %fusion.37), channel_id=1, source_target_pairs={{1,0},{2,1},{3,2},{4,3},{5,4},{6,5},{7,6},{8,7},{9,8},{10,9},{11,1... | collective-permute-start | bytes 786440 | tf_op jit(solution)/shard_map/ppermute | solution.py:14
Sparse Core Ops, SparseCore 0:
  45.6 104.1 all-reduce.1
where the time goes:
time: 159 us
  waiting for transfers between devices  110 us (69%)
  between operations  14.3 us (9%)
  local copies, waits for them, and re-layouts  10.4 us (7%)
  matrix products  10.2 us (6%)
  starting transfers between devices  9.75 us (6%)
  other arithmetic  4.31 us (3%)
    psum x1, waiting for transfers between devices, on_device(): whole = lax.psum(term, ('ctx', 'dp'))  101 us
    ppermute x3, starting transfers between devices, shifted(): return lax.ppermute(block, axis, route)  9.71 us
    ppermute x3, waiting for transfers between devices, shifted(): return lax.ppermute(block, axis, route)  9.19 us
    unnamed x10, local copies, waits for them, and re-layouts  8.33 us
  transfers between devices with their start and end apart: 4, of which 2 were waited for; matrix products, arithmetic and copies ran while one was open for 8% of the time, Pallas kernels for 0%

commit v1 on v0

--- a/solution.py
+++ b/solution.py
@@ -12,6 +12,51 @@
     devices = range(lax.axis_size(axis))
     route = [(i - distance, i) for i in devices if i - distance in devices]
     return lax.ppermute(block, axis, route)
+
+
+def exchange(block, axis, bit):
+    count = lax.axis_size(axis)
+    return lax.ppermute(block, axis, [(i, i ^ bit) for i in range(count)])
+
+
+def halving_scatter(chunks, axis):
+    count = lax.axis_size(axis)
+    place = lax.axis_index(axis)
+    bit = 1
+    while bit < count:
+        pairs = chunks.reshape((chunks.shape[0] // 2, 2) + chunks.shape[1:])
+        side = (place // bit) % 2
+        kept = lax.dynamic_index_in_dim(pairs, side, 1, keepdims=False)
+        sent = lax.dynamic_index_in_dim(pairs, 1 - side, 1, keepdims=False)
+        chunks = kept + exchange(sent, axis, bit)
+        bit *= 2
+    return chunks[0]
+
+
+def doubling_gather(chunk, axis):
+    count = lax.axis_size(axis)
+    place = lax.axis_index(axis)
+    held = chunk[None]
+    bit = count // 2
+    while bit >= 1:
+        other = exchange(held, axis, bit)
+        side = (place // bit) % 2
+        low = jnp.where(side == 0, held, other)
+        high = jnp.where(side == 0, other, held)
+        held = jnp.stack([low, high], 1).reshape((held.shape[0] * 2,) + held.shape[1:])
+        bit //= 2
+    return held
+
+
+def spread_sum(term):
+    ctx_count = lax.axis_size("ctx")
+    dp_count = lax.axis_size("dp")
+    cols = term.shape[1]
+    piece = term.shape[0] // (ctx_count * dp_count)
+    by_ctx = term.reshape(dp_count, ctx_count, piece, cols).transpose(1, 0, 2, 3)
+    over_ctx = halving_scatter(by_ctx, "ctx")
+    over_all = halving_scatter(over_ctx, "dp")
+    return doubling_gather(over_all, "ctx").reshape(ctx_count * piece, cols)
 
 
 def window_grads(block_of_query, key_span_window, value_span_window, block_gradient, visible):
@@ -61,9 +106,13 @@
 
 
 def weight_term(hidden_block, kv_grad):
-    return jnp.einsum(
-        "td,tc->dc", hidden_block.astype(jnp.float32), kv_grad, precision=lax.Precision.HIGHEST
+    high = kv_grad.astype(jnp.bfloat16)
+    low = (kv_grad - high.astype(jnp.float32)).astype(jnp.bfloat16)
+    both = jnp.einsum(
+        "td,tc->dc", hidden_block, jnp.concatenate([high, low], 1), preferred_element_type=jnp.float32
     )
+    cols = kv_grad.shape[1]
+    return both[:, :cols] + both[:, cols:]
 
 
 def on_device(hidden_in, queries, keys, values, out_grad, segment_ids):
@@ -94,9 +143,7 @@
     term = weight_term(hidden_in, kv_window[rows_per_block:] + returned)
     total_rows = term.shape[0]
     replica_count = lax.axis_size("dp")
-    whole = lax.psum(term, ("ctx", "dp"))
-    share = total_rows // replica_count
-    weight_grad = lax.dynamic_slice_in_dim(whole, lax.axis_index("dp") * share, share, 0)
+    weight_grad = spread_sum(term)
     return (query_grad.astype(jnp.bfloat16), weight_grad)
 
 

time: 159 us -> 109 us (0.69)
  waiting for transfers between devices: 110 us -> 54.4 us
  between operations: 14.3 us -> 1.08 us
  other arithmetic: 4.31 us -> 14.3 us
  starting transfers between devices: 9.75 us -> 16 us
  local copies, waits for them, and re-layouts: 10.4 us -> 16.1 us
  matrix products: 10.2 us -> 6.69 us
    psum x1 -> x0, waiting for transfers between devices: 101 us -> none  [on_device(): whole = lax.psum(term, ('ctx', 'dp'))]
    ppermute x0 -> x6, waiting for transfers between devices: none -> 45.2 us  [exchange(): return lax.ppermute(block, axis, [(i, i ^ bit) for i in range(count)])]
    add x0 -> x5, other arithmetic: none -> 7.85 us  [the longest x4 5.59 us: halving_scatter(): chunks = kept + exchange(sent, axis, bit)]
    ppermute x0 -> x6, starting transfers between devices: none -> 6.32 us  [exchange(): return lax.ppermute(block, axis, [(i, i ^ bit) for i in range(count)])]
    add x0 -> x1, local copies, waits for them, and re-layouts: none -> 3.53 us  [weight_term(): return both[:, :cols] + both[:, cols:]]
    dynamic_slice x1 -> x2, local copies, waits for them, and re-layouts: 1.18 us -> 3.46 us  [the longest x1 3.34 us: halving_scatter(): kept = lax.dynamic_index_in_dim(pairs, side, 1, keepdims=False)]
    dot_general x1, matrix products: 3.1 us -> 0.98 us  [weight_term(): jnp.einsum('td,tc->dc', hidden_block, jnp.concatenate([high, low], 1), pr...]
    another operation x1 -> x4, other arithmetic: 0.04 us -> 2.07 us  [the longest x3 2.03 us: doubling_gather(): jnp.stack([low, high], 1).reshape((held.shape[0] * 2,) + held.shape[1:])]
  transfers between devices with their start and end apart: 4 -> 9, of which waited for: 2 -> 6; matrix products, arithmetic and copies ran while one was open for 8% -> 11% of each run, Pallas kernels for 0% -> 0%
where the time goes in v1:
time: 109 us
  waiting for transfers between devices  54.4 us (50%)
  local copies, waits for them, and re-layouts  16.1 us (15%)
  starting transfers between devices  16 us (15%)
  other arithmetic  14.3 us (13%)
  matrix products  6.69 us (6%)
    ppermute x6, waiting for transfers between devices, exchange(): return lax.ppermute(block, axis, [(i, i ^ bit) for i in range(count)])  45.2 us
    ppermute x3, starting transfers between devices, shifted(): return lax.ppermute(block, axis, route)  9.71 us
    ppermute x3, waiting for transfers between devices, shifted(): return lax.ppermute(block, axis, route)  9.21 us
    unnamed x17, local copies, waits for them, and re-layouts  7.38 us
    ppermute x6, starting transfers between devices, exchange(): return lax.ppermute(block, axis, [(i, i ^ bit) for i in range(count)])  6.32 us
    add x4, other arithmetic, halving_scatter(): chunks = kept + exchange(sent, axis, bit)  5.59 us
    add x1, local copies, waits for them, and re-layouts, weight_term(): return both[:, :cols] + both[:, cols:]  3.53 us
    dynamic_slice x1, local copies, waits for them, and re-layouts, halving_scatter(): kept = lax.dynamic_index_in_dim(pairs, side, 1, keepdims=False)  3.34 us
  transfers between devices with their start and end apart: 9, of which 6 were waited for; matrix products, arithmetic and copies ran while one was open for 11% of the time, Pallas kernels for 0%

profile of v1, /device:TPU:0, one launch (start us, length us, event | category | flops | bytes accessed | tf_op | source)
XLA Modules:
  0.0 108.6 jit_solution(2240605714795941661)
XLA Ops:
  0.6 1.1 copy.27
  1.7 4.9 %collective-permute-start.1 = (bf16[256,256]{0,1:T(8,128)(2,1)S(1)}, bf16[256,256]{0,1:T(8,128)(2,1)S(1)}, u32[]{:S(2)}, u32[]{:S(2)}) collective-permute-start(bf16[256,256]{0,1:T(8,128)(2,1)S(1)} %copy.27), channel_id=1, source_target_pairs={{0,1},{1,2},{2,3},{3,4},{4,5},{5,6},{6,7},{7,8},{8,9},{9,10},{10,1... | collective-permute-start | bytes 393224 | tf_op jit(solution)/shard_map/ppermute | solution.py:14
  7.7 3.5 %collective-permute-start = (bf16[256,256]{0,1:T(8,128)(2,1)S(1)}, bf16[256,256]{0,1:T(8,128)(2,1)S(1)}, u32[]{:S(2)}, u32[]{:S(2)}) collective-permute-start(bf16[256,256]{0,1:T(8,128)(2,1)S(1)} %copy.22), channel_id=1, source_target_pairs={{0,1},{1,2},{2,3},{3,4},{4,5},{5,6},{6,7},{7,8},{8,9},{9,10},{10,1... | collective-permute-start | bytes 393224 | tf_op jit(solution)/shard_map/ppermute | solution.py:14
  11.2 1.4 %copy.25 = bf16[256,1536]{0,1:T(8,128)(2,1)S(1)} copy(bf16[256,1536]{1,0:T(8,128)(2,1)} %param.7) | data formatting | bytes 1572864 | tf_op args[1]
  12.6 1.4 %copy.30 = bf16[256,1536]{0,1:T(8,128)(2,1)S(1)} copy(bf16[256,1536]{1,0:T(8,128)(2,1)} %param.10) | data formatting | bytes 1572864 | tf_op args[4]
  16.3 1.4 %fusion.55 = (f32[6,256]{1,0:T(8,128)S(1)}, f32[6,256,512]{1,2,0:T(8,128)S(1)}) fusion(f32[512,256,6]{1,0,2:T(8,128)S(1)} %fusion.44, pred[256,512]{0,1:T(8,128)(4,1)S(1)} %fusion.41), kind=kOutput, calls=%fused_computation.103 | output fusion | flops 4719103 | bytes 6428672 | tf_op jit(solution)/shard_map/sub | solution.py:85
  18.4 1.5 %fusion.56 = (f32[6,256]{1,0:T(8,128)S(1)}, f32[6,256,512]{1,2,0:T(8,128)S(1)}) fusion(f32[512,256,6]{1,0,2:T(8,128)S(1)} %fusion.42, pred[256,512]{0,1:T(8,128)(4,1)S(1)} %fusion.41), kind=kOutput, calls=%fused_computation.104 | output fusion | flops 4719103 | bytes 6428672 | tf_op jit(solution)/shard_map/sub | solution.py:85
  24.8 1.3 %collective-permute-start.2 = (bf16[256,512]{0,1:T(8,128)(2,1)S(1)}, bf16[256,512]{0,1:T(8,128)(2,1)S(1)}, u32[]{:S(2)}, u32[]{:S(2)}) collective-permute-start(bf16[256,512]{0,1:T(8,128)(2,1)S(1)} %fusion.36), channel_id=1, source_target_pairs={{1,0},{2,1},{3,2},{4,3},{5,4},{6,5},{7,6},{8,7},{9,8},{10,9},{11,1... | collective-permute-start | bytes 786440 | tf_op jit(solution)/shard_map/ppermute | solution.py:14
  26.1 9.2 %collective-permute-done.2 = bf16[256,512]{0,1:T(8,128)(2,1)S(1)} collective-permute-done((bf16[256,512]{0,1:T(8,128)(2,1)S(1)}, bf16[256,512]{0,1:T(8,128)(2,1)S(1)}, u32[]{:S(2)}, u32[]{:S(2)}) %collective-permute-start.2) | collective-permute-done | bytes 262176 | tf_op jit(solution)/shard_map/ppermute | solution.py:14
  36.4 2.3 %slice_add_fusion = f32[1536,512]{0,1:T(8,128)} fusion(f32[1536,1024]{0,1:T(8,128)S(1)} %convolution_bitcast_fusion), kind=kLoop, calls=%fused_computation.3 | loop fusion | flops 786432 | bytes 9437184 | tf_op jit(solution)/shard_map/add | solution.py:115
  38.7 3.5 %copy.48 = f32[1536,512]{1,0:T(8,128)} copy(f32[1536,512]{0,1:T(8,128)} %slice_add_fusion) | data formatting | bytes 6291456 | tf_op jit(solution)/shard_map/add | solution.py:115
  42.2 3.3 %constant_dynamic-slice_fusion.3 = (f32[2,1,4,96,512]{4,3,1,0,2:T(8,128)}, f32[2,1,4,96,512]{4,3,1,0,2:T(8,128)S(1)}) fusion(f32[2,2,4,96,512]{4,3,1,0,2:T(8,128)} %bitcast.176, s32[]{:T(128)S(6)} %select_n.108, s32[]{:T(128)S(6)} %select_n.109), kind=kLoop, calls=%fused_computation.92 | loop fusion | bytes 6291464 | tf_op jit(solution)/shard_map/jit(dynamic_index_in_dim)/dynamic_slice | solution.py:29
  45.8 3.5 %collective-permute-done.3 = f32[2,4,96,512]{3,2,1,0:T(8,128)} collective-permute-done((f32[2,4,96,512]{3,2,1,0:T(8,128)S(1)}, f32[2,4,96,512]{3,2,1,0:T(8,128)}, u32[]{:S(2)}, u32[]{:S(2)}) %collective-permute-start.3) | collective-permute-done | bytes 1572896 | tf_op jit(solution)/shard_map/ppermute | solution.py:19
  49.3 2.3 %bitcast_add_fusion = f32[2,4,96,512]{3,2,1,0:T(8,128)S(1)} fusion(f32[2,4,96,512]{3,2,1,0:T(8,128)} %collective-permute-done.3, f32[2,1,4,96,512]{4,3,1,0,2:T(8,128)} %get-tuple-element.8), kind=kLoop, calls=%fused_computation.20 | loop fusion | flops 393216 | bytes 4718592 | tf_op jit(solution)/shard_map/add | solution.py:31
  51.7 1.6 %collective-permute-start.4 = (f32[1,4,96,512]{3,2,1,0:T(8,128)S(1)}, f32[1,4,96,512]{3,2,1,0:T(8,128)}, u32[]{:S(2)}, u32[]{:S(2)}) collective-permute-start(f32[1,4,96,512]{3,2,1,0:T(8,128)S(1)} %constant_dynamic-slice_fusion.1), channel_id=1, source_target_pairs={{0,8},{4,12},{8,0},{12,4},{1,9},{5,13},{9,1},{13,5},{2,10},{6,14},... | collective-permute-start | bytes 2359304 | tf_op jit(solution)/shard_map/ppermute | solution.py:19
  53.3 18.1 %collective-permute-done.4 = f32[1,4,96,512]{3,2,1,0:T(8,128)} collective-permute-done((f32[1,4,96,512]{3,2,1,0:T(8,128)S(1)}, f32[1,4,96,512]{3,2,1,0:T(8,128)}, u32[]{:S(2)}, u32[]{:S(2)}) %collective-permute-start.4) | collective-permute-done | bytes 786464 | tf_op jit(solution)/shard_map/ppermute | solution.py:19
  71.4 1.3 %dynamic-slice_add_fusion = f32[1,4,96,512]{3,2,1,0:T(8,128)S(1)} fusion(f32[1,4,96,512]{3,2,1,0:T(8,128)} %collective-permute-done.4, f32[2,4,96,512]{3,2,1,0:T(8,128)S(1)} %bitcast_add_fusion, s32[]{:T(128)S(6)} %select_n.110), kind=kLoop, calls=%fused_computation.52 | loop fusion | flops 196608 | bytes 2359300 | tf_op jit(solution)/shard_map/add | solution.py:31
  73.9 10.2 %collective-permute-done.5 = f32[2,96,512]{2,1,0:T(8,128)} collective-permute-done((f32[2,96,512]{2,1,0:T(8,128)}, f32[2,96,512]{2,1,0:T(8,128)}, u32[]{:S(2)}, u32[]{:S(2)}) %collective-permute-start.5) | collective-permute-done | bytes 393248 | tf_op jit(solution)/shard_map/ppermute | solution.py:19
  84.1 1.0 bitcast_add_fusion.1
  86.0 3.2 %collective-permute-start.6 = (f32[1,96,512]{2,1,0:T(8,128)S(1)}, f32[1,96,512]{2,1,0:T(8,128)S(1)}, u32[]{:S(2)}, u32[]{:S(2)}) collective-permute-start(f32[1,96,512]{2,1,0:T(8,128)S(1)} %constant_dynamic-slice_fusion), channel_id=1, source_target_pairs={{0,2},{1,3},{2,0},{3,1},{4,6},{5,7},{6,4},{7,5},{8,10},{9,11},{10,... | collective-permute-start | bytes 589832 | tf_op jit(solution)/shard_map/ppermute | solution.py:19
  89.2 8.2 %collective-permute-done.6 = f32[1,96,512]{2,1,0:T(8,128)S(1)} collective-permute-done((f32[1,96,512]{2,1,0:T(8,128)S(1)}, f32[1,96,512]{2,1,0:T(8,128)S(1)}, u32[]{:S(2)}, u32[]{:S(2)}) %collective-permute-start.6) | collective-permute-done | bytes 196640 | tf_op jit(solution)/shard_map/ppermute | solution.py:19
  99.3 5.1 %collective-permute-done.7 = f32[1,96,512]{2,1,0:T(8,128)S(1)} collective-permute-done((f32[1,96,512]{2,1,0:T(8,128)S(1)}, f32[1,96,512]{2,1,0:T(8,128)S(1)}, u32[]{:S(2)}, u32[]{:S(2)}) %collective-permute-start.7) | collective-permute-done | bytes 196640 | tf_op jit(solution)/shard_map/ppermute | solution.py:19
  105.4 1.2 %copy.52 = bf16[256,1536]{1,0:T(8,128)(2,1)} copy(bf16[256,1536]{0,1:T(8,128)(2,1)S(1)} %bitcast.187) | data formatting | bytes 1572864
  106.6 1.1 select_bitcast_fusion.1
  (53 shorter events, 15.7 us)
Async XLA Ops:
  0.6 34.8 %copy-start = (bf16[256,1536]{1,0:T(8,128)(2,1)S(1)}, bf16[256,1536]{1,0:T(8,128)(2,1)}, u32[]{:S(2)}) copy-start(bf16[256,1536]{1,0:T(8,128)(2,1)} %param.6) | copy-start | bytes 2359300
  1.7 18.1 %collective-permute-start.1 = (bf16[256,256]{0,1:T(8,128)(2,1)S(1)}, bf16[256,256]{0,1:T(8,128)(2,1)S(1)}, u32[]{:S(2)}, u32[]{:S(2)}) collective-permute-start(bf16[256,256]{0,1:T(8,128)(2,1)S(1)} %copy.27), channel_id=1, source_target_pairs={{0,1},{1,2},{2,3},{3,4},{4,5},{5,6},{6,7},{7,8},{8,9},{9,10},{10,1... | collective-permute-start | bytes 393224 | tf_op jit(solution)/shard_map/ppermute | solution.py:14
  7.7 7.4 %collective-permute-start = (bf16[256,256]{0,1:T(8,128)(2,1)S(1)}, bf16[256,256]{0,1:T(8,128)(2,1)S(1)}, u32[]{:S(2)}, u32[]{:S(2)}) collective-permute-start(bf16[256,256]{0,1:T(8,128)(2,1)S(1)} %copy.22), channel_id=1, source_target_pairs={{0,1},{1,2},{2,3},{3,4},{4,5},{5,6},{6,7},{7,8},{8,9},{9,10},{10,1... | collective-permute-start | bytes 393224 | tf_op jit(solution)/shard_map/ppermute | solution.py:14
  22.3 1.2 %copy-start.1 = (bf16[6,256,512]{1,2,0:T(8,128)(2,1)}, bf16[6,256,512]{1,2,0:T(8,128)(2,1)S(1)}, u32[]{:S(2)}) copy-start(bf16[6,256,512]{1,2,0:T(8,128)(2,1)S(1)} %fusion.4) | copy-start | bytes 4718596
  23.4 1.2 %copy-start.3 = (bf16[6,256,512]{1,2,0:T(8,128)(2,1)}, bf16[6,256,512]{1,2,0:T(8,128)(2,1)S(1)}, u32[]{:S(2)}) copy-start(bf16[6,256,512]{1,2,0:T(8,128)(2,1)S(1)} %fusion.7) | copy-start | bytes 4718596
  24.8 10.5 %collective-permute-start.2 = (bf16[256,512]{0,1:T(8,128)(2,1)S(1)}, bf16[256,512]{0,1:T(8,128)(2,1)S(1)}, u32[]{:S(2)}, u32[]{:S(2)}) collective-permute-start(bf16[256,512]{0,1:T(8,128)(2,1)S(1)} %fusion.36), channel_id=1, source_target_pairs={{1,0},{2,1},{3,2},{4,3},{5,4},{6,5},{7,6},{8,7},{9,8},{10,9},{11,1... | collective-permute-start | bytes 786440 | tf_op jit(solution)/shard_map/ppermute | solution.py:14
  45.7 3.6 %collective-permute-start.3 = (f32[2,4,96,512]{3,2,1,0:T(8,128)S(1)}, f32[2,4,96,512]{3,2,1,0:T(8,128)}, u32[]{:S(2)}, u32[]{:S(2)}) collective-permute-start(f32[2,4,96,512]{3,2,1,0:T(8,128)S(1)} %bitcast.192), channel_id=1, source_target_pairs={{0,4},{4,0},{8,12},{12,8},{1,5},{5,1},{9,13},{13,9},{2,6},{6,2},{1... | collective-permute-start | bytes 4718600 | tf_op jit(solution)/shard_map/ppermute | solution.py:19
  51.7 19.8 %collective-permute-start.4 = (f32[1,4,96,512]{3,2,1,0:T(8,128)S(1)}, f32[1,4,96,512]{3,2,1,0:T(8,128)}, u32[]{:S(2)}, u32[]{:S(2)}) collective-permute-start(f32[1,4,96,512]{3,2,1,0:T(8,128)S(1)} %constant_dynamic-slice_fusion.1), channel_id=1, source_target_pairs={{0,8},{4,12},{8,0},{12,4},{1,9},{5,13},{9,1},{13,5},{2,10},{6,14},... | collective-permute-start | bytes 2359304 | tf_op jit(solution)/shard_map/ppermute | solution.py:19
  72.7 31.8 %copy-start.2 = (bf16[6,256,512]{1,2,0:T(8,128)(2,1)S(1)}, bf16[6,256,512]{1,2,0:T(8,128)(2,1)}, u32[]{:S(2)}) copy-start(bf16[6,256,512]{1,2,0:T(8,128)(2,1)} %copy-done.1) | copy-start | bytes 4718596
  73.5 10.6 %collective-permute-start.5 = (f32[2,96,512]{2,1,0:T(8,128)}, f32[2,96,512]{2,1,0:T(8,128)}, u32[]{:S(2)}, u32[]{:S(2)}) collective-permute-start(f32[2,96,512]{2,1,0:T(8,128)} %dynamic-slice_bitcast_fusion), channel_id=1, source_target_pairs={{0,1},{1,0},{2,3},{3,2},{4,5},{5,4},{6,7},{7,6},{8,9},{9,8},{10,11... | collective-permute-start | bytes 1179656 | tf_op jit(solution)/shard_map/ppermute | solution.py:19
  85.2 0.7 copy-start.5
  86.0 11.5 %collective-permute-start.6 = (f32[1,96,512]{2,1,0:T(8,128)S(1)}, f32[1,96,512]{2,1,0:T(8,128)S(1)}, u32[]{:S(2)}, u32[]{:S(2)}) collective-permute-start(f32[1,96,512]{2,1,0:T(8,128)S(1)} %constant_dynamic-slice_fusion), channel_id=1, source_target_pairs={{0,2},{1,3},{2,0},{3,1},{4,6},{5,7},{6,4},{7,5},{8,10},{9,11},{10,... | collective-permute-start | bytes 589832 | tf_op jit(solution)/shard_map/ppermute | solution.py:19
  98.4 6.0 %collective-permute-start.7 = (f32[1,96,512]{2,1,0:T(8,128)S(1)}, f32[1,96,512]{2,1,0:T(8,128)S(1)}, u32[]{:S(2)}, u32[]{:S(2)}) collective-permute-start(f32[1,96,512]{2,1,0:T(8,128)S(1)} %dynamic-slice_add_fusion.1), channel_id=1, source_target_pairs={{0,8},{4,12},{8,0},{12,4},{1,9},{5,13},{9,1},{13,5},{2,10},{6,14},... | collective-permute-start | bytes 589832 | tf_op jit(solution)/shard_map/ppermute | solution.py:19
  99.3 5.6 %copy-start.4 = (bf16[6,256,512]{1,2,0:T(8,128)(2,1)S(1)}, bf16[6,256,512]{1,2,0:T(8,128)(2,1)}, u32[]{:S(2)}) copy-start(bf16[6,256,512]{1,2,0:T(8,128)(2,1)} %copy-done.3) | copy-start | bytes 4718596
  104.4 2.1 %collective-permute-start.8 = (f32[2,96,512]{2,1,0:T(8,128)S(1)}, f32[2,96,512]{2,1,0:T(8,128)}, u32[]{:S(2)}, u32[]{:S(2)}) collective-permute-start(f32[2,96,512]{2,1,0:T(8,128)S(1)} %maximum_bitcast_fusion), channel_id=1, source_target_pairs={{0,4},{4,0},{8,12},{12,8},{1,5},{5,1},{9,13},{13,9},{2,6},{6,2},{1... | collective-permute-start | bytes 1179656 | tf_op jit(solution)/shard_map/ppermute | solution.py:19

commit v2 on v1

--- a/solution.py
+++ b/solution.py
@@ -19,18 +19,27 @@
     return lax.ppermute(block, axis, [(i, i ^ bit) for i in range(count)])
 
 
-def halving_scatter(chunks, axis):
+def bits_of(count):
+    width = count.bit_length() - 1
+    assert 1 << width == count
+    return width
+
+
+def halving_scatter(chunks, axis, first_sent=None):
     count = lax.axis_size(axis)
     place = lax.axis_index(axis)
     bit = 1
     while bit < count:
-        pairs = chunks.reshape((chunks.shape[0] // 2, 2) + chunks.shape[1:])
         side = (place // bit) % 2
-        kept = lax.dynamic_index_in_dim(pairs, side, 1, keepdims=False)
-        sent = lax.dynamic_index_in_dim(pairs, 1 - side, 1, keepdims=False)
+        if first_sent is None:
+            kept = lax.dynamic_index_in_dim(chunks, side, 0, keepdims=False)
+            sent = lax.dynamic_index_in_dim(chunks, 1 - side, 0, keepdims=False)
+        else:
+            kept, sent = chunks, first_sent
+            first_sent = None
         chunks = kept + exchange(sent, axis, bit)
         bit *= 2
-    return chunks[0]
+    return chunks
 
 
 def doubling_gather(chunk, axis):
@@ -48,14 +57,77 @@
     return held
 
 
-def spread_sum(term):
+def split_hi_lo(values):
+    high = values.astype(jnp.bfloat16)
+    rest = values - lax.reduce_precision(values, exponent_bits=8, mantissa_bits=7)
+    return jnp.concatenate([high, rest.astype(jnp.bfloat16)], 1)
+
+
+def weight_rows(hidden_cols, kv_parts):
+    both = jnp.einsum("td,tc->dc", hidden_cols, kv_parts, preferred_element_type=jnp.float32)
+    cols = kv_parts.shape[1] // 2
+    return both[:, :cols] + both[:, cols:]
+
+
+def routed_scatter(halves, labels, schedules):
+    labels = [list(labels) for _ in halves]
+    halves = list(halves)
+    for step in range(len(schedules[0])):
+        sends = {}
+        for h, schedule in enumerate(schedules):
+            axis, bit = schedule[step]
+            at = labels[h].index((axis, bit))
+            side = (lax.axis_index(axis) // bit) % 2
+            kept = lax.dynamic_index_in_dim(halves[h], side, at, keepdims=False)
+            sent = lax.dynamic_index_in_dim(halves[h], 1 - side, at, keepdims=False)
+            labels[h].pop(at)
+            halves[h] = kept
+            sends.setdefault((axis, bit), []).append((h, sent))
+        for (axis, bit), items in sends.items():
+            if len(items) == 1:
+                got = [exchange(items[0][1], axis, bit)]
+            else:
+                got = exchange(jnp.stack([x for _, x in items]), axis, bit)
+                got = [got[k] for k in range(len(items))]
+            for (h, _), g in zip(items, got):
+                halves[h] = halves[h] + g
+    return halves
+
+
+def weight_grad_of(hidden_window, kv_window):
     ctx_count = lax.axis_size("ctx")
     dp_count = lax.axis_size("dp")
-    cols = term.shape[1]
-    piece = term.shape[0] // (ctx_count * dp_count)
-    by_ctx = term.reshape(dp_count, ctx_count, piece, cols).transpose(1, 0, 2, 3)
-    over_ctx = halving_scatter(by_ctx, "ctx")
-    over_all = halving_scatter(over_ctx, "dp")
+    ctx_bits = bits_of(ctx_count)
+    dp_bits = bits_of(dp_count)
+    tokens, width = hidden_window.shape
+    cols = kv_window.shape[1]
+    piece = width // (ctx_count * dp_count)
+    split = hidden_window.reshape((tokens,) + (2,) * (dp_bits + ctx_bits) + (piece,))
+    d_axes = list(range(1, 1 + dp_bits))
+    c_axes = list(range(1 + dp_bits, 1 + dp_bits + ctx_bits))
+    order = [0] + c_axes[::-1] + d_axes[::-1] + [1 + dp_bits + ctx_bits]
+    hidden_cols = split.transpose(order).reshape(tokens, 2, width // 2)
+    kv_parts = split_hi_lo(kv_window)
+    side = lax.axis_index("ctx") % 2
+    sent_cols = lax.dynamic_index_in_dim(hidden_cols, 1 - side, 1, keepdims=False)
+    kept_cols = lax.dynamic_index_in_dim(hidden_cols, side, 1, keepdims=False)
+    lead = (2,) * (ctx_bits + dp_bits - 1) + (piece, cols)
+    sent = weight_rows(sent_cols, kv_parts).reshape(lead)
+    kept = weight_rows(kept_cols, kv_parts).reshape(lead)
+    summed = kept + exchange(sent, "ctx", 1)
+    ctx_rest = [("ctx", 1 << k) for k in range(1, ctx_bits)]
+    dp_all = [("dp", 1 << k) for k in range(dp_bits)]
+    labels = ctx_rest + dp_all
+    if dp_all and ctx_rest:
+        first = ctx_rest + dp_all
+        second = dp_all[:1] + ctx_rest + dp_all[1:]
+        half = cols // 2
+        parts = routed_scatter(
+            [summed[..., :half], summed[..., half:]], labels, [first, second]
+        )
+        over_all = jnp.concatenate(parts, -1)
+    else:
+        over_all = routed_scatter([summed], labels, [labels])[0]
     return doubling_gather(over_all, "ctx").reshape(ctx_count * piece, cols)
 
 
@@ -105,22 +177,14 @@
     return (query_grad, jnp.concatenate([key_gradient, value_gradient], 1))
 
 
-def weight_term(hidden_block, kv_grad):
-    high = kv_grad.astype(jnp.bfloat16)
-    low = (kv_grad - high.astype(jnp.float32)).astype(jnp.bfloat16)
-    both = jnp.einsum(
-        "td,tc->dc", hidden_block, jnp.concatenate([high, low], 1), preferred_element_type=jnp.float32
-    )
-    cols = kv_grad.shape[1]
-    return both[:, :cols] + both[:, cols:]
-
-
 def on_device(hidden_in, queries, keys, values, out_grad, segment_ids):
     rows_per_block = queries.shape[0]
     cycle_place = lax.axis_index(("ctx", "dp"))
-    prev_keys, prev_values = shifted((keys, values), ("ctx", "dp"), 1)
-    key_span_window = jnp.concatenate([prev_keys, keys], 0)
-    value_span_window = jnp.concatenate([prev_values, values], 0)
+    kv_width = keys.shape[1]
+    prev_kv = shifted(jnp.concatenate([keys, values], 1), ("ctx", "dp"), 1)
+    prev_hidden = shifted(hidden_in, ("ctx", "dp"), 1)
+    key_span_window = jnp.concatenate([prev_kv[:, :kv_width], keys], 0)
+    value_span_window = jnp.concatenate([prev_kv[:, kv_width:], values], 0)
     own_segments = lax.dynamic_slice_in_dim(
         segment_ids, cycle_place * rows_per_block, rows_per_block, 0
     )
@@ -137,13 +201,8 @@
     query_grad, kv_window = window_grads(
         queries, key_span_window, value_span_window, out_grad, visible
     )
-    returned = shifted(kv_window[:rows_per_block].astype(jnp.bfloat16), ("ctx", "dp"), -1).astype(
-        jnp.float32
-    )
-    term = weight_term(hidden_in, kv_window[rows_per_block:] + returned)
-    total_rows = term.shape[0]
-    replica_count = lax.axis_size("dp")
-    weight_grad = spread_sum(term)
+    hidden_window = jnp.concatenate([prev_hidden, hidden_in], 0)
+    weight_grad = weight_grad_of(hidden_window, kv_window)
     return (query_grad.astype(jnp.bfloat16), weight_grad)
 
 

time: 109 us -> 95.5 us (0.88)
  waiting for transfers between devices: 54.4 us -> 35.3 us
  other arithmetic: 14.3 us -> 19.2 us
  matrix products: 6.69 us -> 9.15 us
  local copies, waits for them, and re-layouts: 16.1 us -> 14 us
    ppermute x6 -> x8, waiting for transfers between devices: 45.2 us -> 31.7 us  [exchange(): return lax.ppermute(block, axis, [(i, i ^ bit) for i in range(count)])]
    ppermute x3 -> x2, waiting for transfers between devices: 9.21 us -> 3.65 us  [shifted(): return lax.ppermute(block, axis, route)]
    dynamic_slice x3 -> x2, local copies, waits for them, and re-layouts: 4.31 us -> 0.03 us  [routed_scatter(): sent = lax.dynamic_index_in_dim(halves[h], 1 - side, at, keepdims=False)]
    add x1 -> x0, local copies, waits for them, and re-layouts: 3.53 us -> none  [weight_term(): return both[:, :cols] + both[:, cols:]]
    unnamed x17 -> x40, local copies, waits for them, and re-layouts: 7.38 us -> 10.2 us
    dot_general x1 -> x2, matrix products: 0.98 us -> 3.46 us  [weight_rows(): jnp.einsum('td,tc->dc', hidden_cols, kv_parts, preferred_element_type=jnp...]
    squeeze x3 -> x4, local copies, waits for them, and re-layouts: 0.85 us -> 2.62 us  [routed_scatter(): sent = lax.dynamic_index_in_dim(halves[h], 1 - side, at, keepdims=False)]
    concatenate x2 -> x3, other arithmetic: 0.04 us -> 1.53 us  [the longest x1 1.48 us: on_device(): hidden_window = jnp.concatenate([prev_hidden, hidden_in], 0)]
  transfers between devices with their start and end apart: 9 -> 10, of which waited for: 6 -> 8; matrix products, arithmetic and copies ran while one was open for 11% -> 23% of each run, Pallas kernels for 0% -> 0%
where the time goes in v2:
time: 95.5 us; the launch traced here: 94.9 us
  waiting for transfers between devices  35.3 us (37%)
  other arithmetic  19.2 us (20%)
  starting transfers between devices  16 us (17%)
  local copies, waits for them, and re-layouts  14 us (15%)
  matrix products  9.15 us (10%)
  between operations  1.16 us (1%)
    ppermute x8, waiting for transfers between devices, exchange(): return lax.ppermute(block, axis, [(i, i ^ bit) for i in range(count)])  31.7 us
    unnamed x40, local copies, waits for them, and re-layouts  10.2 us
    ppermute x2, starting transfers between devices, shifted(): return lax.ppermute(block, axis, route)  9.29 us
    ppermute x8, starting transfers between devices, exchange(): return lax.ppermute(block, axis, [(i, i ^ bit) for i in range(count)])  6.74 us
    ppermute x2, waiting for transfers between devices, shifted(): return lax.ppermute(block, axis, route)  3.65 us
    dot_general x2, matrix products, weight_rows(): jnp.einsum('td,tc->dc', hidden_cols, kv_parts, preferred_element_type=jnp...  3.46 us
    add x5, other arithmetic, routed_scatter(): halves[h] = halves[h] + g  3.44 us
    sub x2, other arithmetic, window_grads(): expo = jnp.exp(scores - top)  3.07 us
  transfers between devices with their start and end apart: 10, of which 8 were waited for; matrix products, arithmetic and copies ran while one was open for 23% of the time, Pallas kernels for 0%

profile of v2, /device:TPU:0, one launch (start us, length us, event | category | flops | bytes accessed | tf_op | source)
XLA Modules:
  0.0 94.9 jit_solution(1520711015676310588)
XLA Ops:
  0.7 1.1 %copy.22 = bf16[256,256]{0,1:T(8,128)(2,1)S(1)} copy(bf16[256,256]{1,0:T(8,128)(2,1)} %param.8) | data formatting | bytes 262144 | tf_op args[2]
  2.8 4.9 %collective-permute-start = (bf16[256,512]{0,1:T(8,128)(2,1)S(1)}, bf16[256,512]{0,1:T(8,128)(2,1)S(1)}, u32[]{:S(2)}, u32[]{:S(2)}) collective-permute-start(bf16[256,512]{0,1:T(8,128)(2,1)S(1)} %pad_maximum_fusion.9), channel_id=1, source_target_pairs={{0,1},{1,2},{2,3},{3,4},{4,5},{5,6},{6,7},{7,8},{8,9},{9,10},{10,1... | collective-permute-start | bytes 786440 | tf_op jit(solution)/shard_map/ppermute | solution.py:14
  7.8 2.3 %copy.40 = bf16[256,1536]{0,1:T(8,128)(2,1)} copy(bf16[256,1536]{1,0:T(8,128)(2,1)} %param.6) | data formatting | bytes 1572864 | tf_op args[0]
  10.1 4.3 %collective-permute-start.1 = (bf16[256,1536]{0,1:T(8,128)(2,1)}, bf16[256,1536]{0,1:T(8,128)(2,1)}, u32[]{:S(2)}, u32[]{:S(2)}) collective-permute-start(bf16[256,1536]{0,1:T(8,128)(2,1)} %copy.40), channel_id=1, source_target_pairs={{0,1},{1,2},{2,3},{3,4},{4,5},{5,6},{6,7},{7,8},{8,9},{9,10},{10,1... | collective-permute-start | bytes 2359304 | tf_op jit(solution)/shard_map/ppermute | solution.py:14
  17.4 1.6 %fusion.63 = (f32[6,256]{1,0:T(8,128)S(1)}, f32[6,256,512]{1,2,0:T(8,128)S(1)}) fusion(f32[512,256,6]{1,0,2:T(8,128)S(1)} %fusion.44, pred[256,512]{0,1:T(8,128)(4,1)S(1)} %fusion.43), kind=kOutput, calls=%fused_computation.117 | output fusion | flops 4719103 | bytes 6428672 | tf_op jit(solution)/shard_map/sub | solution.py:157
  21.4 1.4 %fusion.62 = (f32[6,256]{1,0:T(8,128)S(1)}, f32[6,256,512]{1,2,0:T(8,128)S(1)}) fusion(f32[512,256,6]{1,0,2:T(8,128)S(1)} %fusion.46, pred[256,512]{0,1:T(8,128)(4,1)S(1)} %fusion.43), kind=kOutput, calls=%fused_computation.116 | output fusion | flops 4719103 | bytes 6428672 | tf_op jit(solution)/shard_map/sub | solution.py:157
  26.7 3.6 %collective-permute-done.1 = bf16[256,1536]{0,1:T(8,128)(2,1)} collective-permute-done((bf16[256,1536]{0,1:T(8,128)(2,1)}, bf16[256,1536]{0,1:T(8,128)(2,1)}, u32[]{:S(2)}, u32[]{:S(2)}) %collective-permute-start.1) | collective-permute-done | bytes 786464 | tf_op jit(solution)/shard_map/ppermute | solution.py:14
  30.3 1.5 %pad_maximum_fusion = bf16[512,1536]{0,1:T(8,128)(2,1)S(1)} fusion(bf16[256,1536]{0,1:T(8,128)(2,1)} %copy.40, bf16[256,1536]{0,1:T(8,128)(2,1)} %collective-permute-done.1), kind=kLoop, calls=%fused_computation.20 | loop fusion | flops 3145728 | bytes 3145728 | tf_op jit(solution)/shard_map/concatenate | solution.py:204
  33.1 1.5 %slice_add_fusion = f32[768,512]{1,0:T(8,128)} fusion(f32[768,1024]{1,0:T(8,128)S(1)} %fusion.36), kind=kLoop, calls=%fused_computation.18 | loop fusion | flops 393216 | bytes 4718592 | tf_op jit(solution)/shard_map/add | solution.py:69
  34.6 2.4 %collective-permute-start.2 = (f32[2,2,2,96,512]{4,3,2,1,0:T(8,128)}, f32[2,2,2,96,512]{4,3,2,1,0:T(8,128)}, u32[]{:S(2)}, u32[]{:S(2)}) collective-permute-start(f32[2,2,2,96,512]{4,3,2,1,0:T(8,128)} %bitcast.43), channel_id=1, source_target_pairs={{0,4},{4,0},{8,12},{12,8},{1,5},{5,1},{9,13},{13,9},{2,6},{6,2},{1... | collective-permute-start | bytes 4718600 | tf_op jit(solution)/shard_map/ppermute | solution.py:19
  37.0 2.4 %fusion.38 = f32[768,1024]{1,0:T(8,128)S(1)} fusion(bf16[512,2,768]{0,2,1:T(8,128)(2,1)} %bitcast.214, s32[]{:T(128)S(6)} %select_n.123, bf16[512,512]{0,1:T(8,128)(2,1)} %copy-done.16, bf16[512,512]{0,1:T(8,128)(2,1)} %copy-done.15), kind=kOutput, calls=%fused_computation.56 | convolution fusion | flops 807403520 | bytes 4980740 | tf_op jit(solution)/shard_map/td,tc->dc/dot_general | solution.py:67
  40.4 1.8 %add.126 = f32[2,2,2,96,512]{4,3,2,1,0:T(8,128)S(1)} add(f32[2,2,2,96,512]{4,3,2,1,0:T(8,128)S(1)} %bitcast.199, f32[2,2,2,96,512]{4,3,2,1,0:T(8,128)} %collective-permute-done.2) | non-fusion elementwise | flops 393216 | bytes 4718592 | tf_op jit(solution)/shard_map/add | solution.py:117
  44.8 3.0 %collective-permute-start.3 = (f32[2,2,96,256]{3,2,1,0:T(8,128)}, f32[2,2,96,256]{3,2,1,0:T(8,128)}, u32[]{:S(2)}, u32[]{:S(2)}) collective-permute-start(f32[2,2,96,256]{3,2,1,0:T(8,128)} %dynamic-slice_bitcast_fusion.1), channel_id=1, source_target_pairs={{0,8},{4,12},{8,0},{12,4},{1,9},{5,13},{9,1},{13,5},{2,10},{6,14},... | collective-permute-start | bytes 1179656 | tf_op jit(solution)/shard_map/ppermute | solution.py:19
  47.8 1.8 %dynamic-slice_bitcast_fusion = f32[2,2,96,256]{3,2,1,0:T(8,128)} fusion(f32[2,2,2,96,256]{4,3,2,1,0:T(8,128)} %get-tuple-element.7, s32[]{:T(128)S(6)} %select_n.129), kind=kLoop, calls=%fused_computation.74 | loop fusion | bytes 786436 | tf_op jit(solution)/shard_map/jit(dynamic_index_in_dim)/squeeze | solution.py:82
  49.6 8.0 %collective-permute-done.3 = f32[2,2,96,256]{3,2,1,0:T(8,128)} collective-permute-done((f32[2,2,96,256]{3,2,1,0:T(8,128)}, f32[2,2,96,256]{3,2,1,0:T(8,128)}, u32[]{:S(2)}, u32[]{:S(2)}) %collective-permute-start.3) | collective-permute-done | bytes 393248 | tf_op jit(solution)/shard_map/ppermute | solution.py:19
  57.5 1.2 %bitcast_add_fusion.1 = f32[2,2,96,256]{3,2,1,0:T(8,128)S(1)} fusion(f32[2,2,96,256]{3,2,1,0:T(8,128)} %collective-permute-done.3, f32[2,2,2,96,256]{4,3,2,1,0:T(8,128)} %copy-done.2, s32[]{:T(128)S(6)} %select_n.125), kind=kLoop, calls=%fused_computation.71 | loop fusion | flops 98304 | bytes 1179652 | tf_op jit(solution)/shard_map/add | solution.py:93
  58.8 2.0 %collective-permute-done.5 = f32[2,2,96,256]{3,2,1,0:T(8,128)} collective-permute-done((f32[2,2,96,256]{3,2,1,0:T(8,128)}, f32[2,2,96,256]{3,2,1,0:T(8,128)}, u32[]{:S(2)}, u32[]{:S(2)}) %collective-permute-start.5) | collective-permute-done | bytes 393248 | tf_op jit(solution)/shard_map/ppermute | solution.py:19
  60.8 1.2 %bitcast_add_fusion = f32[2,2,96,256]{3,2,1,0:T(8,128)S(1)} fusion(f32[2,2,96,256]{3,2,1,0:T(8,128)} %collective-permute-done.5, f32[2,2,2,96,256]{4,3,2,1,0:T(8,128)} %get-tuple-element.7, s32[]{:T(128)S(6)} %select_n.128), kind=kLoop, calls=%fused_computation.70 | loop fusion | flops 98304 | bytes 1179652 | tf_op jit(solution)/shard_map/add | solution.py:93
  62.3 2.9 %collective-permute-done.4 = f32[2,96,256]{2,1,0:T(8,128)S(1)} collective-permute-done((f32[2,96,256]{2,1,0:T(8,128)S(1)}, f32[2,96,256]{2,1,0:T(8,128)S(1)}, u32[]{:S(2)}, u32[]{:S(2)}) %collective-permute-start.4) | collective-permute-done | bytes 196640 | tf_op jit(solution)/shard_map/ppermute | solution.py:19
  65.3 2.5 %collective-permute-done.6 = f32[2,96,256]{2,1,0:T(8,128)S(1)} collective-permute-done((f32[2,96,256]{2,1,0:T(8,128)S(1)}, f32[2,96,256]{2,1,0:T(8,128)S(1)}, u32[]{:S(2)}, u32[]{:S(2)}) %collective-permute-start.6) | collective-permute-done | bytes 196640 | tf_op jit(solution)/shard_map/ppermute | solution.py:19
  69.2 10.3 %collective-permute-done.7 = f32[2,96,256]{2,1,0:T(8,128)} collective-permute-done((f32[2,96,256]{2,1,0:T(8,128)}, f32[2,96,256]{2,1,0:T(8,128)}, u32[]{:S(2)}, u32[]{:S(2)}) %collective-permute-start.7) | collective-permute-done | bytes 196640 | tf_op jit(solution)/shard_map/ppermute | solution.py:19
  82.9 5.4 %collective-permute-done.8 = f32[1,96,512]{2,1,0:T(8,128)} collective-permute-done((f32[1,96,512]{2,1,0:T(8,128)}, f32[1,96,512]{2,1,0:T(8,128)}, u32[]{:S(2)}, u32[]{:S(2)}) %collective-permute-start.8) | collective-permute-done | bytes 196640 | tf_op jit(solution)/shard_map/ppermute | solution.py:19
  91.7 1.2 %copy.54 = bf16[256,1536]{1,0:T(8,128)(2,1)} copy(bf16[256,1536]{0,1:T(8,128)(2,1)S(1)} %bitcast.208) | data formatting | bytes 1572864
  92.9 1.1 %select_bitcast_fusion.1 = (f32[2,1,96,512]{3,2,1,0:T(8,128)S(1)}, f32[2,1,96,512]{3,2,1,0:T(8,128)S(1)}) fusion(f32[2,96,512]{2,1,0:T(8,128)} %collective-permute-done.9, pred[]{:T(512)S(6)} %eq.38, f32[1,1,96,512]{3,2,1,0:T(8,128)S(1)} %copy-done.6, f32[1,1,96,512]{3,2,1,0:T(8,128)S(1)} %copy-done.4), kind=kLoop, calls=%fused_computation.73 | loop fusion | flops 294912 | bytes 1572865 | tf_op jit(solution)/shard_map/stack | solution.py:55
  (87 shorter events, 24.4 us)
Async XLA Ops:
  0.6 14.6 %copy-start.9 = (bf16[256,1536]{1,0:T(8,128)(2,1)S(1)}, bf16[256,1536]{1,0:T(8,128)(2,1)}, u32[]{:S(2)}) copy-start(bf16[256,1536]{1,0:T(8,128)(2,1)} %param.7) | copy-start | bytes 2359300
  0.6 14.9 %copy-start.10 = (bf16[256,1536]{1,0:T(8,128)(2,1)S(1)}, bf16[256,1536]{1,0:T(8,128)(2,1)}, u32[]{:S(2)}) copy-start(bf16[256,1536]{1,0:T(8,128)(2,1)} %param.10) | copy-start | bytes 2359300
  2.8 13.3 %collective-permute-start = (bf16[256,512]{0,1:T(8,128)(2,1)S(1)}, bf16[256,512]{0,1:T(8,128)(2,1)S(1)}, u32[]{:S(2)}, u32[]{:S(2)}) collective-permute-start(bf16[256,512]{0,1:T(8,128)(2,1)S(1)} %pad_maximum_fusion.9), channel_id=1, source_target_pairs={{0,1},{1,2},{2,3},{3,4},{4,5},{5,6},{6,7},{7,8},{8,9},{9,10},{10,1... | collective-permute-start | bytes 786440 | tf_op jit(solution)/shard_map/ppermute | solution.py:14
  10.1 20.3 %collective-permute-start.1 = (bf16[256,1536]{0,1:T(8,128)(2,1)}, bf16[256,1536]{0,1:T(8,128)(2,1)}, u32[]{:S(2)}, u32[]{:S(2)}) collective-permute-start(bf16[256,1536]{0,1:T(8,128)(2,1)} %copy.40), channel_id=1, source_target_pairs={{0,1},{1,2},{2,3},{3,4},{4,5},{5,6},{6,7},{7,8},{8,9},{9,10},{10,1... | collective-permute-start | bytes 2359304 | tf_op jit(solution)/shard_map/ppermute | solution.py:14
  15.6 5.2 %copy-start = (bf16[256,1536]{0,1:T(8,128)(2,1)}, bf16[256,1536]{0,1:T(8,128)(2,1)S(1)}, u32[]{:S(2)}) copy-start(bf16[256,1536]{0,1:T(8,128)(2,1)S(1)} %copy.26) | copy-start | bytes 2359300
  15.8 7.0 %copy-start.11 = (bf16[256,1536]{0,1:T(8,128)(2,1)}, bf16[256,1536]{0,1:T(8,128)(2,1)S(1)}, u32[]{:S(2)}) copy-start(bf16[256,1536]{0,1:T(8,128)(2,1)S(1)} %copy.30) | copy-start | bytes 2359300
  23.5 1.1 %copy-start.1 = (bf16[256,1536]{0,1:T(8,128)(2,1)S(1)}, bf16[256,1536]{0,1:T(8,128)(2,1)}, u32[]{:S(2)}) copy-start(bf16[256,1536]{0,1:T(8,128)(2,1)} %copy-done) | copy-start | bytes 2359300
  24.6 1.1 %copy-start.12 = (bf16[256,1536]{0,1:T(8,128)(2,1)S(1)}, bf16[256,1536]{0,1:T(8,128)(2,1)}, u32[]{:S(2)}) copy-start(bf16[256,1536]{0,1:T(8,128)(2,1)} %copy-done.11) | copy-start | bytes 2359300
  26.5 5.4 %copy-start.15 = (bf16[512,512]{0,1:T(8,128)(2,1)}, bf16[512,512]{0,1:T(8,128)(2,1)S(1)}, u32[]{:S(2)}) copy-start(bf16[512,512]{0,1:T(8,128)(2,1)S(1)} %fusion.35) | copy-start | bytes 1572868
  26.7 5.3 %copy-start.16 = (bf16[512,512]{0,1:T(8,128)(2,1)}, bf16[512,512]{0,1:T(8,128)(2,1)S(1)}, u32[]{:S(2)}) copy-start(bf16[512,512]{0,1:T(8,128)(2,1)S(1)} %fusion.34) | copy-start | bytes 1572868
  31.9 1.2 %copy-start.7 = (bf16[512,2,2,2,2,96]{0,5,4,3,2,1:T(8,128)(2,1)}, bf16[512,2,2,2,2,96]{0,5,4,3,2,1:T(8,128)(2,1)S(1)}, u32[]{:S(2)}) copy-start(bf16[512,2,2,2,2,96]{0,5,4,3,2,1:T(8,128)(2,1)S(1)} %copy.42) | copy-start | bytes 4718596
  34.6 5.8 %collective-permute-start.2 = (f32[2,2,2,96,512]{4,3,2,1,0:T(8,128)}, f32[2,2,2,96,512]{4,3,2,1,0:T(8,128)}, u32[]{:S(2)}, u32[]{:S(2)}) collective-permute-start(f32[2,2,2,96,512]{4,3,2,1,0:T(8,128)} %bitcast.43), channel_id=1, source_target_pairs={{0,4},{4,0},{8,12},{12,8},{1,5},{5,1},{9,13},{13,9},{2,6},{6,2},{1... | collective-permute-start | bytes 4718600 | tf_op jit(solution)/shard_map/ppermute | solution.py:19
  43.2 0.9 copy-start.2
  44.8 12.7 %collective-permute-start.3 = (f32[2,2,96,256]{3,2,1,0:T(8,128)}, f32[2,2,96,256]{3,2,1,0:T(8,128)}, u32[]{:S(2)}, u32[]{:S(2)}) collective-permute-start(f32[2,2,96,256]{3,2,1,0:T(8,128)} %dynamic-slice_bitcast_fusion.1), channel_id=1, source_target_pairs={{0,8},{4,12},{8,0},{12,4},{1,9},{5,13},{9,1},{13,5},{2,10},{6,14},... | collective-permute-start | bytes 1179656 | tf_op jit(solution)/shard_map/ppermute | solution.py:19
  49.6 11.2 %collective-permute-start.5 = (f32[2,2,96,256]{3,2,1,0:T(8,128)}, f32[2,2,96,256]{3,2,1,0:T(8,128)}, u32[]{:S(2)}, u32[]{:S(2)}) collective-permute-start(f32[2,2,96,256]{3,2,1,0:T(8,128)} %dynamic-slice_bitcast_fusion), channel_id=1, source_target_pairs={{0,1},{1,0},{2,3},{3,2},{4,5},{5,4},{6,7},{7,6},{8,9},{9,8},{10,11... | collective-permute-start | bytes 1179656 | tf_op jit(solution)/shard_map/ppermute | solution.py:19
  58.7 6.5 %collective-permute-start.4 = (f32[2,96,256]{2,1,0:T(8,128)S(1)}, f32[2,96,256]{2,1,0:T(8,128)S(1)}, u32[]{:S(2)}, u32[]{:S(2)}) collective-permute-start(f32[2,96,256]{2,1,0:T(8,128)S(1)} %dynamic-slice_bitcast_fusion.3), channel_id=1, source_target_pairs={{0,1},{1,0},{2,3},{3,2},{4,5},{5,4},{6,7},{7,6},{8,9},{9,8},{10,11... | collective-permute-start | bytes 589832 | tf_op jit(solution)/shard_map/ppermute | solution.py:19
  62.0 5.9 %collective-permute-start.6 = (f32[2,96,256]{2,1,0:T(8,128)S(1)}, f32[2,96,256]{2,1,0:T(8,128)S(1)}, u32[]{:S(2)}, u32[]{:S(2)}) collective-permute-start(f32[2,96,256]{2,1,0:T(8,128)S(1)} %dynamic-slice_bitcast_fusion.2), channel_id=1, source_target_pairs={{0,8},{4,12},{8,0},{12,4},{1,9},{5,13},{9,1},{13,5},{2,10},{6,14},... | collective-permute-start | bytes 589832 | tf_op jit(solution)/shard_map/ppermute | solution.py:19
  65.3 2.6 %copy-start.13 = (f32[2,96,256]{2,1,0:T(8,128)}, f32[2,96,256]{2,1,0:T(8,128)S(1)}, u32[]{:S(2)}) copy-start(f32[2,96,256]{2,1,0:T(8,128)S(1)} %bitcast_add_fusion.3) | copy-start | bytes 589828
  69.2 10.3 %collective-permute-start.7 = (f32[2,96,256]{2,1,0:T(8,128)}, f32[2,96,256]{2,1,0:T(8,128)}, u32[]{:S(2)}, u32[]{:S(2)}) collective-permute-start(f32[2,96,256]{2,1,0:T(8,128)} %pad_maximum_fusion.12), channel_id=1, source_target_pairs={{0,2},{1,3},{2,0},{3,1},{4,6},{5,7},{6,4},{7,5},{8,10},{9,11},{10,... | collective-permute-start | bytes 589832 | tf_op jit(solution)/shard_map/ppermute | solution.py:19
  81.9 6.4 %collective-permute-start.8 = (f32[1,96,512]{2,1,0:T(8,128)}, f32[1,96,512]{2,1,0:T(8,128)}, u32[]{:S(2)}, u32[]{:S(2)}) collective-permute-start(f32[1,96,512]{2,1,0:T(8,128)} %maximum_bitcast_fusion.1), channel_id=1, source_target_pairs={{0,8},{4,12},{8,0},{12,4},{1,9},{5,13},{9,1},{13,5},{2,10},{6,14},... | collective-permute-start | bytes 589832 | tf_op jit(solution)/shard_map/ppermute | solution.py:19
  89.4 1.4 %copy-start.5 = (f32[1,1,96,512]{3,2,1,0:T(8,128)}, f32[1,1,96,512]{3,2,1,0:T(8,128)S(1)}, u32[]{:S(2)}) copy-start(f32[1,1,96,512]{3,2,1,0:T(8,128)S(1)} %get-tuple-element.11) | copy-start | bytes 589828
  90.8 2.1 %collective-permute-start.9 = (f32[2,96,512]{2,1,0:T(8,128)}, f32[2,96,512]{2,1,0:T(8,128)}, u32[]{:S(2)}, u32[]{:S(2)}) collective-permute-start(f32[2,96,512]{2,1,0:T(8,128)} %maximum_bitcast_fusion), channel_id=1, source_target_pairs={{0,4},{4,0},{8,12},{12,8},{1,5},{5,1},{9,13},{13,9},{2,6},{6,2},{1... | collective-permute-start | bytes 1179656 | tf_op jit(solution)/shard_map/ppermute | solution.py:19
  91.2 1.7 %copy-start.4 = (f32[1,1,96,512]{3,2,1,0:T(8,128)S(1)}, f32[1,1,96,512]{3,2,1,0:T(8,128)}, u32[]{:S(2)}) copy-start(f32[1,1,96,512]{3,2,1,0:T(8,128)} %copy-done.3) | copy-start | bytes 589828
  91.2 1.7 %copy-start.6 = (f32[1,1,96,512]{3,2,1,0:T(8,128)S(1)}, f32[1,1,96,512]{3,2,1,0:T(8,128)}, u32[]{:S(2)}) copy-start(f32[1,1,96,512]{3,2,1,0:T(8,128)} %copy-done.5) | copy-start | bytes 589828
  (3 other events, 2.0 us)

commit v3 on v2

--- a/solution.py
+++ b/solution.py
@@ -1,6 +1,8 @@
 import jax
 import jax.numpy as jnp
 from jax import lax
+from jax.experimental import pallas as pl
+from jax.experimental.pallas import tpu as pltpu
 from jax.sharding import PartitionSpec as P
 
 QUERY_HEADS = 12
@@ -131,50 +133,59 @@
     return doubling_gather(over_all, "ctx").reshape(ctx_count * piece, cols)
 
 
-def window_grads(block_of_query, key_span_window, value_span_window, block_gradient, visible):
-    rows_per_block = block_of_query.shape[0]
-    rows_in_span = key_span_window.shape[0]
+def attention_kernel(q_ref, g_ref, k_ref, v_ref, qs_ref, ks_ref, dq_ref, dkv_ref):
+    rows = q_ref.shape[0]
+    span = k_ref.shape[0]
     group_width = QUERY_HEADS // KEY_VALUE_HEADS
     scale = HEAD_SIZE ** (-0.5)
-    heads_of_query = block_of_query.reshape(rows_per_block, KEY_VALUE_HEADS, group_width, HEAD_SIZE)
-    head_gradients = block_gradient.reshape(rows_per_block, KEY_VALUE_HEADS, group_width, HEAD_SIZE)
-    heads_of_key = key_span_window.reshape(rows_in_span, KEY_VALUE_HEADS, HEAD_SIZE)
-    heads_of_value = value_span_window.reshape(rows_in_span, KEY_VALUE_HEADS, HEAD_SIZE)
-    query_parts = []
-    key_pieces = []
-    value_pieces = []
-    for head_position in range(KEY_VALUE_HEADS):
-        query_now = heads_of_query[:, head_position]
-        grad_now = head_gradients[:, head_position]
-        key_now = heads_of_key[:, head_position]
-        value_now = heads_of_value[:, head_position]
-        scores = (
-            jnp.einsum("tgd,sd->gts", query_now, key_now, preferred_element_type=jnp.float32)
-            * scale
-        )
-        scores = jnp.where(visible[None], scores, -jnp.inf)
-        top = jnp.max(scores, axis=-1, keepdims=True)
-        expo = jnp.exp(scores - top)
-        probs = expo / jnp.sum(expo, axis=-1, keepdims=True)
-        probs_low = probs.astype(jnp.bfloat16)
-        dprobs = jnp.einsum("tgd,sd->gts", grad_now, value_now, preferred_element_type=jnp.float32)
-        delta = jnp.sum(probs * dprobs, axis=-1, keepdims=True)
-        dscores_low = (probs * (dprobs - delta)).astype(jnp.bfloat16)
-        value_pieces.append(
-            jnp.einsum("gts,tgd->sd", probs_low, grad_now, preferred_element_type=jnp.float32)
-        )
-        key_pieces.append(
-            jnp.einsum("gts,tgd->sd", dscores_low, query_now, preferred_element_type=jnp.float32)
-            * scale
-        )
-        query_parts.append(
-            jnp.einsum("gts,sd->tgd", dscores_low, key_now, preferred_element_type=jnp.float32)
-            * scale
-        )
-    query_grad = jnp.stack(query_parts, 1).reshape(rows_per_block, QUERY_HEADS * HEAD_SIZE)
-    key_gradient = jnp.stack(key_pieces, 1).reshape(rows_in_span, KEY_VALUE_HEADS * HEAD_SIZE)
-    value_gradient = jnp.stack(value_pieces, 1).reshape(rows_in_span, KEY_VALUE_HEADS * HEAD_SIZE)
-    return (query_grad, jnp.concatenate([key_gradient, value_gradient], 1))
+    row = lax.broadcasted_iota(jnp.int32, (rows, span), 0)
+    col = lax.broadcasted_iota(jnp.int32, (rows, span), 1)
+    visible = (col <= row + rows) & (ks_ref[...] == qs_ref[...])
+    kv_cols = KEY_VALUE_HEADS * HEAD_SIZE
+    for kv_head in range(KEY_VALUE_HEADS):
+        kv_at = pl.ds(kv_head * HEAD_SIZE, HEAD_SIZE)
+        key_now = k_ref[:, kv_at]
+        value_now = v_ref[:, kv_at]
+        key_grad = jnp.zeros((span, HEAD_SIZE), jnp.float32)
+        value_grad = jnp.zeros((span, HEAD_SIZE), jnp.float32)
+        for member in range(group_width):
+            q_at = pl.ds((kv_head * group_width + member) * HEAD_SIZE, HEAD_SIZE)
+            query_now = q_ref[:, q_at]
+            grad_now = g_ref[:, q_at]
+            scores = jnp.einsum("td,sd->ts", query_now, key_now, preferred_element_type=jnp.float32) * scale
+            scores = jnp.where(visible, scores, -jnp.inf)
+            top = jnp.max(scores, axis=-1, keepdims=True)
+            expo = jnp.exp(scores - top)
+            probs = expo / jnp.sum(expo, axis=-1, keepdims=True)
+            dprobs = jnp.einsum("td,sd->ts", grad_now, value_now, preferred_element_type=jnp.float32)
+            delta = jnp.sum(probs * dprobs, axis=-1, keepdims=True)
+            dscores_low = (probs * (dprobs - delta)).astype(jnp.bfloat16)
+            probs_low = probs.astype(jnp.bfloat16)
+            value_grad = value_grad + jnp.einsum("ts,td->sd", probs_low, grad_now, preferred_element_type=jnp.float32)
+            key_grad = key_grad + jnp.einsum("ts,td->sd", dscores_low, query_now, preferred_element_type=jnp.float32)
+            query_grad = jnp.einsum("ts,sd->td", dscores_low, key_now, preferred_element_type=jnp.float32) * scale
+            dq_ref[:, q_at] = query_grad.astype(dq_ref.dtype)
+        dkv_ref[:, kv_at] = key_grad * scale
+        dkv_ref[:, pl.ds(kv_cols + kv_head * HEAD_SIZE, HEAD_SIZE)] = value_grad
+
+
+def window_grads(queries, key_window, value_window, out_grad, query_segments, key_segments):
+    rows = queries.shape[0]
+    span = key_window.shape[0]
+    return pl.pallas_call(
+        attention_kernel,
+        out_shape=(
+            jax.ShapeDtypeStruct(queries.shape, jnp.bfloat16),
+            jax.ShapeDtypeStruct((span, 2 * key_window.shape[1]), jnp.float32),
+        ),
+        in_specs=[pl.BlockSpec(memory_space=pltpu.VMEM)] * 6,
+        out_specs=(pl.BlockSpec(memory_space=pltpu.VMEM), pl.BlockSpec(memory_space=pltpu.VMEM)),
+        cost_estimate=pl.CostEstimate(
+            flops=10 * rows * span * QUERY_HEADS * HEAD_SIZE,
+            transcendentals=rows * span * QUERY_HEADS,
+            bytes_accessed=4 * rows * QUERY_HEADS * HEAD_SIZE * 2 + span * 8 * KEY_VALUE_HEADS * HEAD_SIZE,
+        ),
+    )(queries, out_grad, key_window, value_window, query_segments.reshape(rows, 1), key_segments.reshape(1, span))
 
 
 def on_device(hidden_in, queries, keys, values, out_grad, segment_ids):
@@ -191,19 +202,14 @@
     prev_segments = lax.dynamic_slice_in_dim(
         segment_ids, jnp.maximum(cycle_place - 1, 0) * rows_per_block, rows_per_block, 0
     )
+    prev_segments = jnp.where(cycle_place > 0, prev_segments, -1)
     key_segments = jnp.concatenate([prev_segments, own_segments], 0)
-    query_rows = jnp.arange(rows_per_block, dtype=jnp.int32)[:, None]
-    key_cols = jnp.arange(2 * rows_per_block, dtype=jnp.int32)[None, :]
-    visible = (key_cols <= query_rows + rows_per_block) & (
-        (key_cols >= rows_per_block) | (cycle_place > 0)
-    )
-    visible = visible & (key_segments[None, :] == own_segments[:, None])
     query_grad, kv_window = window_grads(
-        queries, key_span_window, value_span_window, out_grad, visible
+        queries, key_span_window, value_span_window, out_grad, own_segments, key_segments
     )
     hidden_window = jnp.concatenate([prev_hidden, hidden_in], 0)
     weight_grad = weight_grad_of(hidden_window, kv_window)
-    return (query_grad.astype(jnp.bfloat16), weight_grad)
+    return (query_grad, weight_grad)
 
 
 def solution(mesh):

time: 95.5 us -> 79.6 us (0.83)
  Pallas kernels: 0 us -> 11.8 us
  local copies, waits for them, and re-layouts: 14 us -> 2.67 us
  other arithmetic: 19.2 us -> 10.1 us
  matrix products: 9.15 us -> 1.95 us
  starting transfers between devices: 16 us -> 17.6 us
  waiting for transfers between devices: 35.3 us -> 34.2 us
    pallas_call x0 -> x1, Pallas kernels: none -> 11.8 us  [window_grads(): pl.pallas_call(attention_kernel, out_shape=(jax.ShapeDtypeStruct(queries....]
    unnamed x40 -> x5, local copies, waits for them, and re-layouts: 10.2 us -> 1.41 us
    dot_general x10 -> x0, matrix products: 5.7 us -> none  [the longest x2 1.29 us: window_grads(): jnp.einsum('gts,tgd->sd', probs_low, grad_now, preferred_element_type=jnp...]
    add x5, other arithmetic: 3.44 us -> 0.18 us  [routed_scatter(): halves[h] = halves[h] + g]
    sub x2 -> x0, other arithmetic: 3.07 us -> none  [window_grads(): expo = jnp.exp(scores - top)]
    ppermute x2, waiting for transfers between devices: 3.65 us -> 0.75 us  [shifted(): return lax.ppermute(block, axis, route)]
    squeeze x4, local copies, waits for them, and re-layouts: 2.62 us -> 0.11 us  [routed_scatter(): sent = lax.dynamic_index_in_dim(halves[h], 1 - side, at, keepdims=False)]
    ppermute x8, starting transfers between devices: 6.74 us -> 9.09 us  [exchange(): return lax.ppermute(block, axis, [(i, i ^ bit) for i in range(count)])]
  transfers between devices with their start and end apart: 10 -> 10, of which waited for: 8 -> 8; matrix products, arithmetic and copies ran while one was open for 23% -> 10% of each run, Pallas kernels for 0% -> 15%
where the time goes in v3:
time: 79.6 us; the launch traced here: 79.2 us
  waiting for transfers between devices  34.2 us (43%)
  starting transfers between devices  17.6 us (22%)
  Pallas kernels  11.8 us (15%)
  other arithmetic  10.1 us (13%)
  local copies, waits for them, and re-layouts  2.67 us (3%)
  matrix products  1.95 us (2%)
  between operations  0.94 us (1%)
    ppermute x8, waiting for transfers between devices, exchange(): return lax.ppermute(block, axis, [(i, i ^ bit) for i in range(count)])  33.5 us
    pallas_call x1, Pallas kernels, window_grads(): pl.pallas_call(attention_kernel, out_shape=(jax.ShapeDtypeStruct(queries....  11.8 us
    ppermute x8, starting transfers between devices, exchange(): return lax.ppermute(block, axis, [(i, i ^ bit) for i in range(count)])  9.09 us
    ppermute x2, starting transfers between devices, shifted(): return lax.ppermute(block, axis, route)  8.46 us
    dot_general x2, matrix products, weight_rows(): jnp.einsum('td,tc->dc', hidden_cols, kv_parts, preferred_element_type=jnp...  1.95 us
    add x2, other arithmetic, weight_rows(): return both[:, :cols] + both[:, cols:]  1.86 us
    convert_element_type x1, other arithmetic, split_hi_lo(): high = values.astype(jnp.bfloat16)  1.78 us
    add x1, other arithmetic, weight_grad_of(): summed = kept + exchange(sent, 'ctx', 1)  1.75 us
  transfers between devices with their start and end apart: 10, of which 8 were waited for; matrix products, arithmetic and copies ran while one was open for 10% of the time, Pallas kernels for 15%

profile of v3, /device:TPU:0, one launch (start us, length us, event | category | flops | bytes accessed | tf_op | source)
XLA Modules:
  0.0 79.2 jit_solution(5997621752535746717)
XLA Ops:
  0.6 1.0 %pad_maximum_fusion.5 = bf16[256,512]{1,0:T(8,128)(2,1)S(1)} fusion(bf16[256,256]{1,0:T(8,128)(2,1)} %param.9, bf16[256,256]{1,0:T(8,128)(2,1)} %param.8), kind=kLoop, calls=%fused_computation.20 | loop fusion | flops 524288 | bytes 524288 | tf_op jit(solution)/shard_map/concatenate | solution.py:195
  1.7 4.9 %collective-permute-start = (bf16[256,512]{1,0:T(8,128)(2,1)S(1)}, bf16[256,512]{1,0:T(8,128)(2,1)S(1)}, u32[]{:S(2)}, u32[]{:S(2)}) collective-permute-start(bf16[256,512]{1,0:T(8,128)(2,1)S(1)} %pad_maximum_fusion.5), channel_id=1, source_target_pairs={{0,1},{1,2},{2,3},{3,4},{4,5},{5,6},{6,7},{7,8},{8,9},{9,10},{10,1... | collective-permute-start | bytes 786440 | tf_op jit(solution)/shard_map/ppermute | solution.py:16
  6.6 1.4 %copy.10 = bf16[256,1536]{0,1:T(8,128)(2,1)S(1)} copy(bf16[256,1536]{1,0:T(8,128)(2,1)} %param.6) | data formatting | bytes 1572864 | tf_op args[0]
  8.0 3.5 %collective-permute-start.1 = (bf16[256,1536]{0,1:T(8,128)(2,1)S(1)}, bf16[256,1536]{0,1:T(8,128)(2,1)S(1)}, u32[]{:S(2)}, u32[]{:S(2)}) collective-permute-start(bf16[256,1536]{0,1:T(8,128)(2,1)S(1)} %copy.10), channel_id=1, source_target_pairs={{0,1},{1,2},{2,3},{3,4},{4,5},{5,6},{6,7},{7,8},{8,9},{9,10},{10,1... | collective-permute-start | bytes 2359304 | tf_op jit(solution)/shard_map/ppermute | solution.py:16
  11.6 0.8 %dynamic-slice_select_fusion = (s32[256]{0:T(256)S(1)}, s32[256]{0:T(256)S(1)}) fusion(s32[4096]{0:T(1024)} %param.11, s32[]{:T(128)S(6)} %select_n.117, pred[]{:T(512)S(6)} %gt.3, s32[]{:T(128)S(6)} %select_n.115), kind=kLoop, calls=%fused_computation.40 | loop fusion | flops 256 | bytes 4105 | tf_op jit(solution)/shard_map/jit(_where)/select_n | solution.py:205
  12.4 0.8 %copy.9.qs_ref = s32[256,1]{1,0:T(8,128)} copy(s32[256,1]{0,1:T(1,128)S(1)} %bitcast.64) | data formatting | bytes 2048 | tf_op jit(solution)/shard_map/reshape | solution.py:188
  13.8 0.8 %pad_maximum_fusion.6 = (bf16[512,256]{1,0:T(8,128)(2,1)}, bf16[512,256]{1,0:T(8,128)(2,1)}) fusion(bf16[256,256]{1,0:T(8,128)(2,1)S(1)} %copy-done, bf16[256,256]{1,0:T(8,128)(2,1)S(1)} %get-tuple-element.15, bf16[256,256]{1,0:T(8,128)(2,1)S(1)} %copy-done.1, bf16[256,256]{1,0:T(8,128)(2,1)S(1)} %get-tuple-element.14), kind=kLoop, calls=%fused_computation.21 | loop fusion | flops 1048576 | bytes 1048576 | tf_op jit(solution)/shard_map/concatenate | solution.py:197
  14.7 11.8 %shard_map.77 = (bf16[256,1536]{1,0:T(8,128)(2,1)}, f32[512,512]{1,0:T(8,128)}) custom-call(bf16[256,1536]{1,0:T(8,128)(2,1)} %q_ref.1, bf16[256,1536]{1,0:T(8,128)(2,1)} %g_ref.1, bf16[512,256]{1,0:T(8,128)(2,1)} %get-tuple-element.20.k_ref, bf16[512,256]{1,0:T(8,128)(2,1)} %get-tuple-element.21.v_ref, s32[256,1]{1,0:T(8,128)} %copy.9.qs_ref, s32[1,512]{1,0:T(1,128)} %bitcast.65), custom_call_target="tpu_custom_call" | custom-call | flops 2013265920 | bytes 4194304 | tf_op jit(solution)/shard_map/pallas_call | solution.py:175
  26.5 1.8 %fusion.14 = (bf16[512,512]{1,0:T(8,128)(2,1)S(1)}, bf16[512,512]{1,0:T(8,128)(2,1)S(1)}) fusion(f32[512,512]{1,0:T(8,128)} %get-tuple-element.5), kind=kLoop, calls=%fused_computation.44 | loop fusion | flops 1048576 | bytes 2097152 | tf_op jit(solution)/shard_map/convert_element_type | solution.py:63
  29.3 1.0 %fusion.1 = f32[768,1024]{1,0:T(8,128)S(1)} fusion(bf16[512,2,768]{0,2,1:T(8,128)(2,1)S(1)} %bitcast.59, s32[]{:T(128)S(6)} %select_n.125, bf16[512,512]{1,0:T(8,128)(2,1)S(1)} %get-tuple-element.9, bf16[512,512]{1,0:T(8,128)(2,1)S(1)} %get-tuple-element.8), kind=kOutput, calls=%fused_computation.7 | convolution fusion | flops 807403520 | bytes 4980740 | tf_op jit(solution)/shard_map/td,tc->dc/dot_general | solution.py:69
  30.3 1.5 %slice_add_fusion = f32[768,512]{1,0:T(8,128)} fusion(f32[768,1024]{1,0:T(8,128)S(1)} %fusion.1), kind=kLoop, calls=%fused_computation | loop fusion | flops 393216 | bytes 4718592 | tf_op jit(solution)/shard_map/add | solution.py:71
  31.8 3.0 %collective-permute-start.2 = (f32[2,2,2,96,512]{4,3,2,1,0:T(8,128)}, f32[2,2,2,96,512]{4,3,2,1,0:T(8,128)}, u32[]{:S(2)}, u32[]{:S(2)}) collective-permute-start(f32[2,2,2,96,512]{4,3,2,1,0:T(8,128)} %bitcast.8), channel_id=1, source_target_pairs={{0,4},{4,0},{8,12},{12,8},{1,5},{5,1},{9,13},{13,9},{2,6},{6,2},{1... | collective-permute-start | bytes 4718600 | tf_op jit(solution)/shard_map/ppermute | solution.py:21
  34.7 1.0 %fusion.3 = f32[768,1024]{1,0:T(8,128)S(1)} fusion(bf16[512,2,768]{0,2,1:T(8,128)(2,1)S(1)} %bitcast.60, s32[]{:T(128)S(6)} %select_n.124, bf16[512,512]{1,0:T(8,128)(2,1)S(1)} %get-tuple-element.9, bf16[512,512]{1,0:T(8,128)(2,1)S(1)} %get-tuple-element.8), kind=kOutput, calls=%fused_computation.9 | convolution fusion | flops 807403520 | bytes 4980740 | tf_op jit(solution)/shard_map/td,tc->dc/dot_general | solution.py:69
  36.1 2.1 %collective-permute-done.2 = f32[2,2,2,96,512]{4,3,2,1,0:T(8,128)} collective-permute-done((f32[2,2,2,96,512]{4,3,2,1,0:T(8,128)}, f32[2,2,2,96,512]{4,3,2,1,0:T(8,128)}, u32[]{:S(2)}, u32[]{:S(2)}) %collective-permute-start.2) | collective-permute-done | bytes 1572896 | tf_op jit(solution)/shard_map/ppermute | solution.py:21
  38.1 1.8 %add.113 = f32[2,2,2,96,512]{4,3,2,1,0:T(8,128)S(1)} add(f32[2,2,2,96,512]{4,3,2,1,0:T(8,128)S(1)} %bitcast.62, f32[2,2,2,96,512]{4,3,2,1,0:T(8,128)} %collective-permute-done.2) | non-fusion elementwise | flops 393216 | bytes 4718592 | tf_op jit(solution)/shard_map/add | solution.py:119
  40.2 2.6 %collective-permute-start.3 = (f32[2,2,96,256]{3,2,1,0:T(8,128)S(1)}, f32[2,2,96,256]{3,2,1,0:T(8,128)S(1)}, u32[]{:S(2)}, u32[]{:S(2)}) collective-permute-start(f32[2,2,96,256]{3,2,1,0:T(8,128)S(1)} %dynamic-slice_bitcast_fusion.1), channel_id=1, source_target_pairs={{0,8},{4,12},{8,0},{12,4},{1,9},{5,13},{9,1},{13,5},{2,10},{6,14},... | collective-permute-start | bytes 1179656 | tf_op jit(solution)/shard_map/ppermute | solution.py:21
  42.8 8.7 %collective-permute-done.5 = f32[2,2,96,256]{3,2,1,0:T(8,128)S(1)} collective-permute-done((f32[2,2,96,256]{3,2,1,0:T(8,128)S(1)}, f32[2,2,96,256]{3,2,1,0:T(8,128)S(1)}, u32[]{:S(2)}, u32[]{:S(2)}) %collective-permute-start.5) | collective-permute-done | bytes 393248 | tf_op jit(solution)/shard_map/ppermute | solution.py:21
  51.6 2.3 %collective-permute-start.6 = (f32[2,96,256]{2,1,0:T(8,128)S(1)}, f32[2,96,256]{2,1,0:T(8,128)S(1)}, u32[]{:S(2)}, u32[]{:S(2)}) collective-permute-start(f32[2,96,256]{2,1,0:T(8,128)S(1)} %dynamic-slice_bitcast_fusion.2), channel_id=1, source_target_pairs={{0,8},{4,12},{8,0},{12,4},{1,9},{5,13},{9,1},{13,5},{2,10},{6,14},... | collective-permute-start | bytes 589832 | tf_op jit(solution)/shard_map/ppermute | solution.py:21
  54.4 3.9 %collective-permute-done.6 = f32[2,96,256]{2,1,0:T(8,128)S(1)} collective-permute-done((f32[2,96,256]{2,1,0:T(8,128)S(1)}, f32[2,96,256]{2,1,0:T(8,128)S(1)}, u32[]{:S(2)}, u32[]{:S(2)}) %collective-permute-start.6) | collective-permute-done | bytes 196640 | tf_op jit(solution)/shard_map/ppermute | solution.py:21
  58.4 1.6 %collective-permute-done.4 = f32[2,96,256]{2,1,0:T(8,128)S(1)} collective-permute-done((f32[2,96,256]{2,1,0:T(8,128)S(1)}, f32[2,96,256]{2,1,0:T(8,128)S(1)}, u32[]{:S(2)}, u32[]{:S(2)}) %collective-permute-start.4) | collective-permute-done | bytes 196640 | tf_op jit(solution)/shard_map/ppermute | solution.py:21
  60.1 10.0 %collective-permute-done.7 = f32[2,96,256]{2,1,0:T(8,128)S(1)} collective-permute-done((f32[2,96,256]{2,1,0:T(8,128)S(1)}, f32[2,96,256]{2,1,0:T(8,128)S(1)}, u32[]{:S(2)}, u32[]{:S(2)}) %collective-permute-start.7) | collective-permute-done | bytes 196640 | tf_op jit(solution)/shard_map/ppermute | solution.py:21
  70.8 5.5 %collective-permute-done.8 = f32[1,96,512]{2,1,0:T(8,128)S(1)} collective-permute-done((f32[1,96,512]{2,1,0:T(8,128)S(1)}, f32[1,96,512]{2,1,0:T(8,128)S(1)}, u32[]{:S(2)}, u32[]{:S(2)}) %collective-permute-start.8) | collective-permute-done | bytes 196640 | tf_op jit(solution)/shard_map/ppermute | solution.py:21
  76.5 1.7 %collective-permute-done.9 = f32[2,96,512]{2,1,0:T(8,128)S(1)} collective-permute-done((f32[2,96,512]{2,1,0:T(8,128)S(1)}, f32[2,96,512]{2,1,0:T(8,128)S(1)}, u32[]{:S(2)}, u32[]{:S(2)}) %collective-permute-start.9) | collective-permute-done | bytes 393248 | tf_op jit(solution)/shard_map/ppermute | solution.py:21
  78.3 0.9 %pad_maximum_fusion.2 = f32[2,2,96,512]{3,2,1,0:T(8,128)} fusion(f32[2,1,96,512]{3,2,1,0:T(8,128)S(1)} %get-tuple-element.11, f32[2,1,96,512]{3,2,1,0:T(8,128)S(1)} %get-tuple-element.10), kind=kLoop, calls=%fused_computation.6 | loop fusion | flops 196608 | bytes 1572864 | tf_op jit(solution)/shard_map/stack | solution.py:57
  (34 shorter events, 3.8 us)
Async XLA Ops:
  0.6 13.2 %copy-start = (bf16[256,256]{1,0:T(8,128)(2,1)S(1)}, bf16[256,256]{1,0:T(8,128)(2,1)}, u32[]{:S(2)}) copy-start(bf16[256,256]{1,0:T(8,128)(2,1)} %param.8) | copy-start | bytes 393220
  0.6 13.2 %copy-start.1 = (bf16[256,256]{1,0:T(8,128)(2,1)S(1)}, bf16[256,256]{1,0:T(8,128)(2,1)}, u32[]{:S(2)}) copy-start(bf16[256,256]{1,0:T(8,128)(2,1)} %param.9) | copy-start | bytes 393220
  1.7 12.1 %collective-permute-start = (bf16[256,512]{1,0:T(8,128)(2,1)S(1)}, bf16[256,512]{1,0:T(8,128)(2,1)S(1)}, u32[]{:S(2)}, u32[]{:S(2)}) collective-permute-start(bf16[256,512]{1,0:T(8,128)(2,1)S(1)} %pad_maximum_fusion.5), channel_id=1, source_target_pairs={{0,1},{1,2},{2,3},{3,4},{4,5},{5,6},{6,7},{7,8},{8,9},{9,10},{10,1... | collective-permute-start | bytes 786440 | tf_op jit(solution)/shard_map/ppermute | solution.py:16
  8.0 21.0 %collective-permute-start.1 = (bf16[256,1536]{0,1:T(8,128)(2,1)S(1)}, bf16[256,1536]{0,1:T(8,128)(2,1)S(1)}, u32[]{:S(2)}, u32[]{:S(2)}) collective-permute-start(bf16[256,1536]{0,1:T(8,128)(2,1)S(1)} %copy.10), channel_id=1, source_target_pairs={{0,1},{1,2},{2,3},{3,4},{4,5},{5,6},{6,7},{7,8},{8,9},{9,10},{10,1... | collective-permute-start | bytes 2359304 | tf_op jit(solution)/shard_map/ppermute | solution.py:16
  31.8 6.3 %collective-permute-start.2 = (f32[2,2,2,96,512]{4,3,2,1,0:T(8,128)}, f32[2,2,2,96,512]{4,3,2,1,0:T(8,128)}, u32[]{:S(2)}, u32[]{:S(2)}) collective-permute-start(f32[2,2,2,96,512]{4,3,2,1,0:T(8,128)} %bitcast.8), channel_id=1, source_target_pairs={{0,4},{4,0},{8,12},{12,8},{1,5},{5,1},{9,13},{13,9},{2,6},{6,2},{1... | collective-permute-start | bytes 4718600 | tf_op jit(solution)/shard_map/ppermute | solution.py:21
  40.1 11.5 %collective-permute-start.5 = (f32[2,2,96,256]{3,2,1,0:T(8,128)S(1)}, f32[2,2,96,256]{3,2,1,0:T(8,128)S(1)}, u32[]{:S(2)}, u32[]{:S(2)}) collective-permute-start(f32[2,2,96,256]{3,2,1,0:T(8,128)S(1)} %dynamic-slice_bitcast_fusion), channel_id=1, source_target_pairs={{0,1},{1,0},{2,3},{3,2},{4,5},{5,4},{6,7},{7,6},{8,9},{9,8},{10,11... | collective-permute-start | bytes 1179656 | tf_op jit(solution)/shard_map/ppermute | solution.py:21
  40.2 13.7 %collective-permute-start.3 = (f32[2,2,96,256]{3,2,1,0:T(8,128)S(1)}, f32[2,2,96,256]{3,2,1,0:T(8,128)S(1)}, u32[]{:S(2)}, u32[]{:S(2)}) collective-permute-start(f32[2,2,96,256]{3,2,1,0:T(8,128)S(1)} %dynamic-slice_bitcast_fusion.1), channel_id=1, source_target_pairs={{0,8},{4,12},{8,0},{12,4},{1,9},{5,13},{9,1},{13,5},{2,10},{6,14},... | collective-permute-start | bytes 1179656 | tf_op jit(solution)/shard_map/ppermute | solution.py:21
  51.6 6.7 %collective-permute-start.6 = (f32[2,96,256]{2,1,0:T(8,128)S(1)}, f32[2,96,256]{2,1,0:T(8,128)S(1)}, u32[]{:S(2)}, u32[]{:S(2)}) collective-permute-start(f32[2,96,256]{2,1,0:T(8,128)S(1)} %dynamic-slice_bitcast_fusion.2), channel_id=1, source_target_pairs={{0,8},{4,12},{8,0},{12,4},{1,9},{5,13},{9,1},{13,5},{2,10},{6,14},... | collective-permute-start | bytes 589832 | tf_op jit(solution)/shard_map/ppermute | solution.py:21
  54.0 5.9 %collective-permute-start.4 = (f32[2,96,256]{2,1,0:T(8,128)S(1)}, f32[2,96,256]{2,1,0:T(8,128)S(1)}, u32[]{:S(2)}, u32[]{:S(2)}) collective-permute-start(f32[2,96,256]{2,1,0:T(8,128)S(1)} %dynamic-slice_bitcast_fusion.3), channel_id=1, source_target_pairs={{0,1},{1,0},{2,3},{3,2},{4,5},{5,4},{6,7},{7,6},{8,9},{9,8},{10,11... | collective-permute-start | bytes 589832 | tf_op jit(solution)/shard_map/ppermute | solution.py:21
  60.0 10.1 %collective-permute-start.7 = (f32[2,96,256]{2,1,0:T(8,128)S(1)}, f32[2,96,256]{2,1,0:T(8,128)S(1)}, u32[]{:S(2)}, u32[]{:S(2)}) collective-permute-start(f32[2,96,256]{2,1,0:T(8,128)S(1)} %pad_maximum_fusion.8), channel_id=1, source_target_pairs={{0,2},{1,3},{2,0},{3,1},{4,6},{5,7},{6,4},{7,5},{8,10},{9,11},{10,... | collective-permute-start | bytes 589832 | tf_op jit(solution)/shard_map/ppermute | solution.py:21
  70.2 6.2 %collective-permute-start.8 = (f32[1,96,512]{2,1,0:T(8,128)S(1)}, f32[1,96,512]{2,1,0:T(8,128)S(1)}, u32[]{:S(2)}, u32[]{:S(2)}) collective-permute-start(f32[1,96,512]{2,1,0:T(8,128)S(1)} %maximum_bitcast_fusion.1), channel_id=1, source_target_pairs={{0,8},{4,12},{8,0},{12,4},{1,9},{5,13},{9,1},{13,5},{2,10},{6,14},... | collective-permute-start | bytes 589832 | tf_op jit(solution)/shard_map/ppermute | solution.py:21
  76.4 1.8 %collective-permute-start.9 = (f32[2,96,512]{2,1,0:T(8,128)S(1)}, f32[2,96,512]{2,1,0:T(8,128)S(1)}, u32[]{:S(2)}, u32[]{:S(2)}) collective-permute-start(f32[2,96,512]{2,1,0:T(8,128)S(1)} %maximum_bitcast_fusion), channel_id=1, source_target_pairs={{0,4},{4,0},{8,12},{12,8},{1,5},{5,1},{9,13},{13,9},{2,6},{6,2},{1... | collective-permute-start | bytes 1179656 | tf_op jit(solution)/shard_map/ppermute | solution.py:21

commit v4 on v3

v4 whole, which is shorter than its diff:
```python
import functools

import jax
import jax.numpy as jnp
from jax import lax
from jax.experimental import pallas as pl
from jax.experimental.pallas import tpu as pltpu
from jax.sharding import PartitionSpec as P

QUERY_HEADS = 12
KEY_VALUE_HEADS = 2
HEAD_SIZE = 128


def shifted(block, axis, distance):
    devices = range(lax.axis_size(axis))
    route = [(i - distance, i) for i in devices if i - distance in devices]
    return lax.ppermute(block, axis, route)


def exchange(block, axis, bit):
    count = lax.axis_size(axis)
    return lax.ppermute(block, axis, [(i, i ^ bit) for i in range(count)])


def bits_of(count):
    width = count.bit_length() - 1
    assert 1 << width == count
    return width


def halving_scatter(chunks, axis, first_sent=None):
    count = lax.axis_size(axis)
    place = lax.axis_index(axis)
    bit = 1
    while bit < count:
        side = (place // bit) % 2
        if first_sent is None:
            kept = lax.dynamic_index_in_dim(chunks, side, 0, keepdims=False)
            sent = lax.dynamic_index_in_dim(chunks, 1 - side, 0, keepdims=False)
        else:
            kept, sent = chunks, first_sent
            first_sent = None
        chunks = kept + exchange(sent, axis, bit)
        bit *= 2
    return chunks


def doubling_gather(chunk, axis):
    count = lax.axis_size(axis)
    place = lax.axis_index(axis)
    held = chunk[None]
    bit = count // 2
    while bit >= 1:
        other = exchange(held, axis, bit)
        side = (place // bit) % 2
        low = jnp.where(side == 0, held, other)
        high = jnp.where(side == 0, other, held)
        held = jnp.stack([low, high], 1).reshape((held.shape[0] * 2,) + held.shape[1:])
        bit //= 2
    return held


def split_hi_lo(values):
    high = values.astype(jnp.bfloat16)
    rest = values - lax.reduce_precision(values, exponent_bits=8, mantissa_bits=7)
    return jnp.concatenate([high, rest.astype(jnp.bfloat16)], 1)


def weight_rows(hidden_cols, kv_parts):
    both = jnp.einsum("td,tc->dc", hidden_cols, kv_parts, preferred_element_type=jnp.float32)
    cols = kv_parts.shape[1] // 2
    return both[:, :cols] + both[:, cols:]


def chain_scatter(chunks, labels, schedule):
    labels = list(labels)
    for axis, bit in schedule:
        at = labels.index((axis, bit))
        side = (lax.axis_index(axis) // bit) % 2
        kept = lax.dynamic_index_in_dim(chunks, side, at, keepdims=False)
        sent = lax.dynamic_index_in_dim(chunks, 1 - side, at, keepdims=False)
        labels.pop(at)
        chunks = kept + exchange(sent, axis, bit)
    return chunks


def head_weight_grad(hidden_cols, kv_window, schedule, labels, lead):
    kv_parts = split_hi_lo(kv_window)
    side = lax.axis_index("ctx") % 2
    sent_cols = lax.dynamic_index_in_dim(hidden_cols, 1 - side, 1, keepdims=False)
    kept_cols = lax.dynamic_index_in_dim(hidden_cols, side, 1, keepdims=False)
    sent = weight_rows(sent_cols, kv_parts).reshape(lead + (kv_window.shape[1],))
    kept = weight_rows(kept_cols, kv_parts).reshape(lead + (kv_window.shape[1],))
    summed = kept + exchange(sent, "ctx", 1)
    return doubling_gather(chain_scatter(summed, labels, schedule), "ctx")


def ordered_hidden(hidden_window):
    ctx_bits = bits_of(lax.axis_size("ctx"))
    dp_bits = bits_of(lax.axis_size("dp"))
    tokens, width = hidden_window.shape
    piece = width // (1 << (ctx_bits + dp_bits))
    split = hidden_window.reshape((tokens,) + (2,) * (dp_bits + ctx_bits) + (piece,))
    d_axes = list(range(1, 1 + dp_bits))
    c_axes = list(range(1 + dp_bits, 1 + dp_bits + ctx_bits))
    order = [0] + c_axes[::-1] + d_axes[::-1] + [1 + dp_bits + ctx_bits]
    lead = (2,) * (ctx_bits + dp_bits - 1) + (piece,)
    return split.transpose(order).reshape(tokens, 2, width // 2), lead


def schedules():
    ctx_bits = bits_of(lax.axis_size("ctx"))
    dp_bits = bits_of(lax.axis_size("dp"))
    ctx_rest = [("ctx", 1 << k) for k in range(1, ctx_bits)]
    dp_all = [("dp", 1 << k) for k in range(dp_bits)]
    labels = ctx_rest + dp_all
    second = dp_all[:1] + ctx_rest + dp_all[1:]
    return labels, labels, second


def attention_kernel(kv_heads, q_ref, g_ref, k_ref, v_ref, qs_ref, ks_ref, dq_ref, dkv_ref):
    rows = q_ref.shape[0]
    span = k_ref.shape[0]
    group_width = QUERY_HEADS // KEY_VALUE_HEADS
    scale = HEAD_SIZE ** (-0.5)
    key_row = lax.broadcasted_iota(jnp.int32, (span, rows), 0)
    query_col = lax.broadcasted_iota(jnp.int32, (span, rows), 1)
    visible = (key_row <= query_col + rows) & (ks_ref[...] == qs_ref[...])
    kv_cols = len(kv_heads) * HEAD_SIZE
    for slot, kv_head in enumerate(kv_heads):
        kv_at = pl.ds(kv_head * HEAD_SIZE, HEAD_SIZE)
        key_now = k_ref[:, kv_at]
        value_now = v_ref[:, kv_at]
        key_grad = jnp.zeros((span, HEAD_SIZE), jnp.float32)
        value_grad = jnp.zeros((span, HEAD_SIZE), jnp.float32)
        for member in range(group_width):
            q_at = pl.ds((slot * group_width + member) * HEAD_SIZE, HEAD_SIZE)
            query_now = q_ref[:, q_at]
            grad_now = g_ref[:, q_at]
            scores = jnp.einsum("sd,td->st", key_now, query_now, preferred_element_type=jnp.float32) * scale
            scores = jnp.where(visible, scores, -jnp.inf)
            top = jnp.max(scores, axis=0, keepdims=True)
            expo = jnp.exp(scores - top)
            probs = expo / jnp.sum(expo, axis=0, keepdims=True)
            dprobs = jnp.einsum("sd,td->st", value_now, grad_now, preferred_element_type=jnp.float32)
            delta = jnp.sum(probs * dprobs, axis=0, keepdims=True)
            dscores_low = (probs * (dprobs - delta)).astype(jnp.bfloat16)
            probs_low = probs.astype(jnp.bfloat16)
            value_grad = value_grad + jnp.einsum("st,td->sd", probs_low, grad_now, preferred_element_type=jnp.float32)
            key_grad = key_grad + jnp.einsum("st,td->sd", dscores_low, query_now, preferred_element_type=jnp.float32)
            query_grad = jnp.einsum("st,sd->td", dscores_low, key_now, preferred_element_type=jnp.float32) * scale
            dq_ref[:, q_at] = query_grad.astype(dq_ref.dtype)
        dkv_ref[:, pl.ds(slot * HEAD_SIZE, HEAD_SIZE)] = key_grad * scale
        dkv_ref[:, pl.ds(kv_cols + slot * HEAD_SIZE, HEAD_SIZE)] = value_grad


def window_grads(kv_heads, queries, key_window, value_window, out_grad, query_segments, key_segments):
    rows = queries.shape[0]
    span = key_window.shape[0]
    group_width = QUERY_HEADS // KEY_VALUE_HEADS
    q_cols = len(kv_heads) * group_width * HEAD_SIZE
    kv_cols = len(kv_heads) * HEAD_SIZE
    return pl.pallas_call(
        functools.partial(attention_kernel, kv_heads),
        grid=(1,),
        out_shape=(
            jax.ShapeDtypeStruct((rows, q_cols), jnp.bfloat16),
            jax.ShapeDtypeStruct((span, 2 * kv_cols), jnp.float32),
        ),
        in_specs=[
            pl.BlockSpec((rows, q_cols), lambda i: (0, kv_heads[0] // len(kv_heads))),
            pl.BlockSpec((rows, q_cols), lambda i: (0, kv_heads[0] // len(kv_heads))),
        ] + [pl.BlockSpec(memory_space=pltpu.VMEM)] * 4,
        out_specs=(pl.BlockSpec(memory_space=pltpu.VMEM), pl.BlockSpec(memory_space=pltpu.VMEM)),
        cost_estimate=pl.CostEstimate(
            flops=10 * rows * span * q_cols,
            transcendentals=rows * span * len(kv_heads) * group_width,
            bytes_accessed=4 * rows * q_cols * 2 + span * 8 * kv_cols,
        ),
    )(queries, out_grad, key_window, value_window, query_segments.reshape(1, rows), key_segments.reshape(span, 1))


def on_device(hidden_in, queries, keys, values, out_grad, segment_ids):
    rows_per_block = queries.shape[0]
    cycle_place = lax.axis_index(("ctx", "dp"))
    kv_width = keys.shape[1]
    prev_kv = shifted(jnp.concatenate([keys, values], 1), ("ctx", "dp"), 1)
    prev_hidden = shifted(hidden_in, ("ctx", "dp"), 1)
    key_span_window = jnp.concatenate([prev_kv[:, :kv_width], keys], 0)
    value_span_window = jnp.concatenate([prev_kv[:, kv_width:], values], 0)
    own_segments = lax.dynamic_slice_in_dim(
        segment_ids, cycle_place * rows_per_block, rows_per_block, 0
    )
    prev_segments = lax.dynamic_slice_in_dim(
        segment_ids, jnp.maximum(cycle_place - 1, 0) * rows_per_block, rows_per_block, 0
    )
    prev_segments = jnp.where(cycle_place > 0, prev_segments, -1)
    key_segments = jnp.concatenate([prev_segments, own_segments], 0)
    hidden_cols, lead = ordered_hidden(jnp.concatenate([prev_hidden, hidden_in], 0))
    labels, first, second = schedules()
    query_parts, weight_parts = [], []
    for kv_head in range(KEY_VALUE_HEADS):
        query_part, kv_part = window_grads(
            (kv_head,), queries, key_span_window, value_span_window, out_grad, own_segments, key_segments
        )
        query_parts.append(query_part)
        schedule = first if kv_head % 2 == 0 else second
        weight_parts.append(head_weight_grad(hidden_cols, kv_part, schedule, labels, lead))
    rows = weight_parts[0].shape[0] * weight_parts[0].shape[1]
    weight_parts = [w.reshape(rows, 2, HEAD_SIZE) for w in weight_parts]
    weight_grad = jnp.stack(weight_parts, 2).reshape(rows, 2 * KEY_VALUE_HEADS * HEAD_SIZE)
    return (jnp.concatenate(query_parts, 1), weight_grad)


def solution(mesh):
    return jax.shard_map(
        on_device,
        mesh=mesh,
        in_specs=(
            P(("groups", "ctx", "dp"), None),
            P(("groups", "ctx", "dp"), None),
            P(("groups", "ctx", "dp"), None),
            P(("groups", "ctx", "dp"), None),
            P(("groups", "ctx", "dp"), None),
            P("groups"),
        ),
        out_specs=(P(("groups", "ctx", "dp"), None), P(("groups", "dp"), None)),
        check_vma=False,
    )
```

time: 79.6 us -> 73.6 us (0.925)
  waiting for transfers between devices: 34.2 us -> 24.7 us
  other arithmetic: 10.1 us -> 6.88 us
  local copies, waits for them, and re-layouts: 2.67 us -> 5.76 us
  starting transfers between devices: 17.6 us -> 20.1 us
    ppermute x8 -> x12, waiting for transfers between devices: 33.5 us -> 23.9 us  [exchange(): return lax.ppermute(block, axis, [(i, i ^ bit) for i in range(count)])]
    ppermute x8 -> x12, starting transfers between devices: 9.09 us -> 11.6 us  [exchange(): return lax.ppermute(block, axis, [(i, i ^ bit) for i in range(count)])]
    reshape x1 -> x2, local copies, waits for them, and re-layouts: 0.8 us -> 2.38 us  [the longest x1 1.51 us: on_device(): jnp.stack(weight_parts, 2).reshape(rows, 2 * KEY_VALUE_HEADS * HEAD_SIZE)]
    add x6, other arithmetic: 1.93 us -> 0.38 us  [the longest x2 0.23 us: head_weight_grad(): summed = kept + exchange(sent, 'ctx', 1)]
    add x2 -> x4, other arithmetic: 1.86 us -> 0.4 us  [weight_rows(): return both[:, :cols] + both[:, cols:]]
    concatenate x1 -> x2, other arithmetic: 0.12 us -> 1.05 us  [the longest x1 0.93 us: on_device(): return (jnp.concatenate(query_parts, 1), weight_grad)]
    another operation x3 -> x6, other arithmetic: 1.05 us -> 0.15 us  [doubling_gather(): jnp.stack([low, high], 1).reshape((held.shape[0] * 2,) + held.shape[1:])]
    unnamed x5 -> x13, local copies, waits for them, and re-layouts: 1.41 us -> 2.29 us
  transfers between devices with their start and end apart: 10 -> 14, of which waited for: 8 -> 10; matrix products, arithmetic and copies ran while one was open for 10% -> 13% of each run, Pallas kernels for 15% -> 17%
where the time goes in v4:
time: 73.6 us; the launch traced here: 73.3 us
  waiting for transfers between devices  24.7 us (34%)
  starting transfers between devices  20.1 us (27%)
  Pallas kernels  12.5 us (17%)
  other arithmetic  6.88 us (9%)
  local copies, waits for them, and re-layouts  5.76 us (8%)
  matrix products  2.27 us (3%)
  between operations  1.11 us (2%)
    ppermute x12, waiting for transfers between devices, exchange(): return lax.ppermute(block, axis, [(i, i ^ bit) for i in range(count)])  23.9 us
    pallas_call x2, Pallas kernels, window_grads(): pl.pallas_call(functools.partial(attention_kernel, kv_heads), grid=(1,),...  12.5 us
    ppermute x12, starting transfers between devices, exchange(): return lax.ppermute(block, axis, [(i, i ^ bit) for i in range(count)])  11.6 us
    ppermute x2, starting transfers between devices, shifted(): return lax.ppermute(block, axis, route)  8.46 us
    unnamed x13, local copies, waits for them, and re-layouts  2.29 us
    dot_general x4, matrix products, weight_rows(): jnp.einsum('td,tc->dc', hidden_cols, kv_parts, preferred_element_type=jnp...  2.27 us
    reshape x1, local copies, waits for them, and re-layouts, on_device(): jnp.stack(weight_parts, 2).reshape(rows, 2 * KEY_VALUE_HEADS * HEAD_SIZE)  1.51 us
  transfers between devices with their start and end apart: 14, of which 10 were waited for; matrix products, arithmetic and copies ran while one was open for 13% of the time, Pallas kernels for 17%

profile of v4, /device:TPU:0, one launch (start us, length us, event | category | flops | bytes accessed | tf_op | source)
XLA Modules:
  0.0 73.3 jit_solution(5204812633616095652)
XLA Ops:
  0.6 1.0 %pad_maximum_fusion.11 = bf16[256,512]{1,0:T(8,128)(2,1)S(1)} fusion(bf16[256,256]{1,0:T(8,128)(2,1)} %param.9, bf16[256,256]{1,0:T(8,128)(2,1)} %param.8), kind=kLoop, calls=%fused_computation.31 | loop fusion | flops 524288 | bytes 524288 | tf_op jit(solution)/shard_map/concatenate | solution.py:188
  1.7 4.9 %collective-permute-start = (bf16[256,512]{1,0:T(8,128)(2,1)S(1)}, bf16[256,512]{1,0:T(8,128)(2,1)S(1)}, u32[]{:S(2)}, u32[]{:S(2)}) collective-permute-start(bf16[256,512]{1,0:T(8,128)(2,1)S(1)} %pad_maximum_fusion.11), channel_id=1, source_target_pairs={{0,1},{1,2},{2,3},{3,4},{4,5},{5,6},{6,7},{7,8},{8,9},{9,10},{10,1... | collective-permute-start | bytes 786440 | tf_op jit(solution)/shard_map/ppermute | solution.py:18
  6.6 1.4 %copy.12 = bf16[256,1536]{0,1:T(8,128)(2,1)S(1)} copy(bf16[256,1536]{1,0:T(8,128)(2,1)} %param.6) | data formatting | bytes 1572864 | tf_op args[0]
  8.0 3.5 %collective-permute-start.1 = (bf16[256,1536]{0,1:T(8,128)(2,1)S(1)}, bf16[256,1536]{0,1:T(8,128)(2,1)S(1)}, u32[]{:S(2)}, u32[]{:S(2)}) collective-permute-start(bf16[256,1536]{0,1:T(8,128)(2,1)S(1)} %copy.12), channel_id=1, source_target_pairs={{0,1},{1,2},{2,3},{3,4},{4,5},{5,6},{6,7},{7,8},{8,9},{9,10},{10,1... | collective-permute-start | bytes 2359304 | tf_op jit(solution)/shard_map/ppermute | solution.py:18
  12.5 0.9 %copy.10.ks_ref = s32[512,1]{1,0:T(8,128)} copy(s32[512,1]{0,1:T(1,128)S(1)} %bitcast.99) | data formatting | bytes 4096 | tf_op jit(solution)/shard_map/reshape | solution.py:181
  14.3 6.2 %shard_map.77 = (bf16[256,768]{1,0:T(8,128)(2,1)}, f32[512,256]{1,0:T(8,128)}) custom-call(bf16[256,1536]{1,0:T(8,128)(2,1)} %q_ref.3, bf16[256,1536]{1,0:T(8,128)(2,1)} %g_ref.3, bf16[512,256]{1,0:T(8,128)(2,1)} %get-tuple-element.26.k_ref, bf16[512,256]{1,0:T(8,128)(2,1)} %get-tuple-element.27.v_ref, s32[1,256]{1,0:T(1,128)} %bitcast.100, ...), custom_call_target="tpu_custom_call" | custom-call | flops 1006632960 | bytes 2097152 | tf_op jit(solution)/shard_map/pallas_call | solution.py:164
  20.5 6.3 %shard_map.78 = (bf16[256,768]{1,0:T(8,128)(2,1)}, f32[512,256]{1,0:T(8,128)}) custom-call(bf16[256,1536]{1,0:T(8,128)(2,1)} %q_ref.3, bf16[256,1536]{1,0:T(8,128)(2,1)} %g_ref.3, bf16[512,256]{1,0:T(8,128)(2,1)} %get-tuple-element.26.k_ref, bf16[512,256]{1,0:T(8,128)(2,1)} %get-tuple-element.27.v_ref, s32[1,256]{1,0:T(1,128)} %bitcast.101, ...), custom_call_target="tpu_custom_call" | custom-call | flops 1006632960 | bytes 2097152 | tf_op jit(solution)/shard_map/pallas_call | solution.py:164
  26.9 1.3 %fusion.25 = (bf16[512,256]{1,0:T(8,128)(2,1)S(1)}, bf16[512,256]{1,0:T(8,128)(2,1)S(1)}) fusion(f32[512,256]{1,0:T(8,128)} %get-tuple-element.9), kind=kLoop, calls=%fused_computation.65 | loop fusion | flops 524288 | bytes 1048576 | tf_op jit(solution)/shard_map/convert_element_type | solution.py:65
  29.9 3.0 %collective-permute-start.2 = (f32[2,2,2,96,256]{4,3,2,1,0:T(8,128)S(1)}, f32[2,2,2,96,256]{4,3,2,1,0:T(8,128)S(1)}, u32[]{:S(2)}, u32[]{:S(2)}) collective-permute-start(f32[2,2,2,96,256]{4,3,2,1,0:T(8,128)S(1)} %bitcast.98), channel_id=1, source_target_pairs={{0,4},{4,0},{8,12},{12,8},{1,5},{5,1},{9,13},{13,9},{2,6},{6,2},{1... | collective-permute-start | bytes 2359304 | tf_op jit(solution)/shard_map/ppermute | solution.py:23
  35.1 2.7 %collective-permute-start.3 = (f32[2,2,96,256]{3,2,1,0:T(8,128)S(1)}, f32[2,2,96,256]{3,2,1,0:T(8,128)S(1)}, u32[]{:S(2)}, u32[]{:S(2)}) collective-permute-start(f32[2,2,96,256]{3,2,1,0:T(8,128)S(1)} %dynamic-slice_bitcast_fusion.1), channel_id=1, source_target_pairs={{0,8},{4,12},{8,0},{12,4},{1,9},{5,13},{9,1},{13,5},{2,10},{6,14},... | collective-permute-start | bytes 1179656 | tf_op jit(solution)/shard_map/ppermute | solution.py:23
  39.1 0.9 %pad_maximum_fusion.1 = bf16[256,1536]{1,0:T(8,128)(2,1)} fusion(bf16[256,768]{1,0:T(8,128)(2,1)S(1)} %copy-done.4, bf16[256,768]{1,0:T(8,128)(2,1)S(1)} %copy-done.3), kind=kLoop, calls=%fused_computation.5 | loop fusion | flops 1572864 | bytes 1572864 | tf_op jit(solution)/shard_map/concatenate | solution.py:213
  40.0 7.1 %collective-permute-done.3 = f32[2,2,96,256]{3,2,1,0:T(8,128)S(1)} collective-permute-done((f32[2,2,96,256]{3,2,1,0:T(8,128)S(1)}, f32[2,2,96,256]{3,2,1,0:T(8,128)S(1)}, u32[]{:S(2)}, u32[]{:S(2)}) %collective-permute-start.3) | collective-permute-done | bytes 393248 | tf_op jit(solution)/shard_map/ppermute | solution.py:23
  47.3 1.6 %collective-permute-done.9 = f32[2,2,96,256]{3,2,1,0:T(8,128)S(1)} collective-permute-done((f32[2,2,96,256]{3,2,1,0:T(8,128)S(1)}, f32[2,2,96,256]{3,2,1,0:T(8,128)S(1)}, u32[]{:S(2)}, u32[]{:S(2)}) %collective-permute-start.9) | collective-permute-done | bytes 393248 | tf_op jit(solution)/shard_map/ppermute | solution.py:23
  49.0 1.0 %collective-permute-start.10 = (f32[2,96,256]{2,1,0:T(8,128)S(1)}, f32[2,96,256]{2,1,0:T(8,128)S(1)}, u32[]{:S(2)}, u32[]{:S(2)}) collective-permute-start(f32[2,96,256]{2,1,0:T(8,128)S(1)} %dynamic-slice_bitcast_fusion.2), channel_id=1, source_target_pairs={{0,8},{4,12},{8,0},{12,4},{1,9},{5,13},{9,1},{13,5},{2,10},{6,14},... | collective-permute-start | bytes 589832 | tf_op jit(solution)/shard_map/ppermute | solution.py:23
  50.0 3.6 %collective-permute-done.4 = f32[2,96,256]{2,1,0:T(8,128)S(1)} collective-permute-done((f32[2,96,256]{2,1,0:T(8,128)S(1)}, f32[2,96,256]{2,1,0:T(8,128)S(1)}, u32[]{:S(2)}, u32[]{:S(2)}) %collective-permute-start.4) | collective-permute-done | bytes 196640 | tf_op jit(solution)/shard_map/ppermute | solution.py:23
  53.7 1.1 %collective-permute-done.10 = f32[2,96,256]{2,1,0:T(8,128)S(1)} collective-permute-done((f32[2,96,256]{2,1,0:T(8,128)S(1)}, f32[2,96,256]{2,1,0:T(8,128)S(1)}, u32[]{:S(2)}, u32[]{:S(2)}) %collective-permute-start.10) | collective-permute-done | bytes 196640 | tf_op jit(solution)/shard_map/ppermute | solution.py:23
  54.8 1.9 %collective-permute-start.11 = (f32[96,256]{1,0:T(8,128)S(1)}, f32[96,256]{1,0:T(8,128)S(1)}, u32[]{:S(2)}, u32[]{:S(2)}) collective-permute-start(f32[96,256]{1,0:T(8,128)S(1)} %dynamic-slice_bitcast_fusion.4), channel_id=1, source_target_pairs={{0,2},{1,3},{2,0},{3,1},{4,6},{5,7},{6,4},{7,5},{8,10},{9,11},{10,... | collective-permute-start | bytes 294920 | tf_op jit(solution)/shard_map/ppermute | solution.py:23
  56.8 5.5 %collective-permute-done.5 = f32[96,256]{1,0:T(8,128)S(1)} collective-permute-done((f32[96,256]{1,0:T(8,128)S(1)}, f32[96,256]{1,0:T(8,128)S(1)}, u32[]{:S(2)}, u32[]{:S(2)}) %collective-permute-start.5) | collective-permute-done | bytes 98336 | tf_op jit(solution)/shard_map/ppermute | solution.py:23
  62.2 1.4 %collective-permute-start.6 = (f32[1,96,256]{2,1,0:T(8,128)S(1)}, f32[1,96,256]{2,1,0:T(8,128)S(1)}, u32[]{:S(2)}, u32[]{:S(2)}) collective-permute-start(f32[1,96,256]{2,1,0:T(8,128)S(1)} %fusion.15), channel_id=1, source_target_pairs={{0,8},{4,12},{8,0},{12,4},{1,9},{5,13},{9,1},{13,5},{2,10},{6,14},... | collective-permute-start | bytes 294920 | tf_op jit(solution)/shard_map/ppermute | solution.py:23
  64.2 1.2 %collective-permute-start.12 = (f32[1,96,256]{2,1,0:T(8,128)S(1)}, f32[1,96,256]{2,1,0:T(8,128)S(1)}, u32[]{:S(2)}, u32[]{:S(2)}) collective-permute-start(f32[1,96,256]{2,1,0:T(8,128)S(1)} %fusion.14), channel_id=1, source_target_pairs={{0,8},{4,12},{8,0},{12,4},{1,9},{5,13},{9,1},{13,5},{2,10},{6,14},... | collective-permute-start | bytes 294920 | tf_op jit(solution)/shard_map/ppermute | solution.py:23
  65.4 1.6 %collective-permute-done.6 = f32[1,96,256]{2,1,0:T(8,128)S(1)} collective-permute-done((f32[1,96,256]{2,1,0:T(8,128)S(1)}, f32[1,96,256]{2,1,0:T(8,128)S(1)}, u32[]{:S(2)}, u32[]{:S(2)}) %collective-permute-start.6) | collective-permute-done | bytes 98336 | tf_op jit(solution)/shard_map/ppermute | solution.py:23
  67.1 1.9 %collective-permute-done.12 = f32[1,96,256]{2,1,0:T(8,128)S(1)} collective-permute-done((f32[1,96,256]{2,1,0:T(8,128)S(1)}, f32[1,96,256]{2,1,0:T(8,128)S(1)}, u32[]{:S(2)}, u32[]{:S(2)}) %collective-permute-start.12) | collective-permute-done | bytes 98336 | tf_op jit(solution)/shard_map/ppermute | solution.py:23
  69.7 0.9 %collective-permute-done.13 = f32[2,96,256]{2,1,0:T(8,128)S(1)} collective-permute-done((f32[2,96,256]{2,1,0:T(8,128)S(1)}, f32[2,96,256]{2,1,0:T(8,128)S(1)}, u32[]{:S(2)}, u32[]{:S(2)}) %collective-permute-start.13) | collective-permute-done | bytes 196640 | tf_op jit(solution)/shard_map/ppermute | solution.py:23
  71.8 1.5 %reshape.49 = f32[384,512]{1,0:T(8,128)} reshape(f32[384,2,2,128]{3,2,1,0:T(2,128)S(1)} %pad_maximum_fusion.2) | data formatting | bytes 1572864 | tf_op jit(solution)/shard_map/reshape | solution.py:212
  (65 shorter events, 9.7 us)
Async XLA Ops:
  0.6 12.8 %copy-start.1 = (bf16[256,256]{1,0:T(8,128)(2,1)S(1)}, bf16[256,256]{1,0:T(8,128)(2,1)}, u32[]{:S(2)}) copy-start(bf16[256,256]{1,0:T(8,128)(2,1)} %param.8) | copy-start | bytes 393220
  0.6 12.8 %copy-start.2 = (bf16[256,256]{1,0:T(8,128)(2,1)S(1)}, bf16[256,256]{1,0:T(8,128)(2,1)}, u32[]{:S(2)}) copy-start(bf16[256,256]{1,0:T(8,128)(2,1)} %param.9) | copy-start | bytes 393220
  1.7 11.7 %collective-permute-start = (bf16[256,512]{1,0:T(8,128)(2,1)S(1)}, bf16[256,512]{1,0:T(8,128)(2,1)S(1)}, u32[]{:S(2)}, u32[]{:S(2)}) collective-permute-start(bf16[256,512]{1,0:T(8,128)(2,1)S(1)} %pad_maximum_fusion.11), channel_id=1, source_target_pairs={{0,1},{1,2},{2,3},{3,4},{4,5},{5,6},{6,7},{7,8},{8,9},{9,10},{10,1... | collective-permute-start | bytes 786440 | tf_op jit(solution)/shard_map/ppermute | solution.py:18
  8.0 21.0 %collective-permute-start.1 = (bf16[256,1536]{0,1:T(8,128)(2,1)S(1)}, bf16[256,1536]{0,1:T(8,128)(2,1)S(1)}, u32[]{:S(2)}, u32[]{:S(2)}) collective-permute-start(bf16[256,1536]{0,1:T(8,128)(2,1)S(1)} %copy.12), channel_id=1, source_target_pairs={{0,1},{1,2},{2,3},{3,4},{4,5},{5,6},{6,7},{7,8},{8,9},{9,10},{10,1... | collective-permute-start | bytes 2359304 | tf_op jit(solution)/shard_map/ppermute | solution.py:18
  12.5 1.8 %copy-start.5 = (s32[256]{0:T(256)}, s32[256]{0:T(256)S(1)}, u32[]{:S(2)}) copy-start(s32[256]{0:T(256)S(1)} %get-tuple-element.25) | copy-start | bytes 3076
  20.5 6.3 %copy-start = (f32[512,256]{1,0:T(8,128)S(1)}, f32[512,256]{1,0:T(8,128)}, u32[]{:S(2)}) copy-start(f32[512,256]{1,0:T(8,128)} %get-tuple-element.8) | copy-start | bytes 1572868
  29.9 5.0 %collective-permute-start.2 = (f32[2,2,2,96,256]{4,3,2,1,0:T(8,128)S(1)}, f32[2,2,2,96,256]{4,3,2,1,0:T(8,128)S(1)}, u32[]{:S(2)}, u32[]{:S(2)}) collective-permute-start(f32[2,2,2,96,256]{4,3,2,1,0:T(8,128)S(1)} %bitcast.98), channel_id=1, source_target_pairs={{0,4},{4,0},{8,12},{12,8},{1,5},{5,1},{9,13},{13,9},{2,6},{6,2},{1... | collective-permute-start | bytes 2359304 | tf_op jit(solution)/shard_map/ppermute | solution.py:23
  33.6 4.3 %collective-permute-start.8 = (f32[2,2,2,96,256]{4,3,2,1,0:T(8,128)S(1)}, f32[2,2,2,96,256]{4,3,2,1,0:T(8,128)S(1)}, u32[]{:S(2)}, u32[]{:S(2)}) collective-permute-start(f32[2,2,2,96,256]{4,3,2,1,0:T(8,128)S(1)} %bitcast.97), channel_id=1, source_target_pairs={{0,4},{4,0},{8,12},{12,8},{1,5},{5,1},{9,13},{13,9},{2,6},{6,2},{1... | collective-permute-start | bytes 2359304 | tf_op jit(solution)/shard_map/ppermute | solution.py:23
  35.1 12.0 %collective-permute-start.3 = (f32[2,2,96,256]{3,2,1,0:T(8,128)S(1)}, f32[2,2,96,256]{3,2,1,0:T(8,128)S(1)}, u32[]{:S(2)}, u32[]{:S(2)}) collective-permute-start(f32[2,2,96,256]{3,2,1,0:T(8,128)S(1)} %dynamic-slice_bitcast_fusion.1), channel_id=1, source_target_pairs={{0,8},{4,12},{8,0},{12,4},{1,9},{5,13},{9,1},{13,5},{2,10},{6,14},... | collective-permute-start | bytes 1179656 | tf_op jit(solution)/shard_map/ppermute | solution.py:23
  38.0 1.0 %copy-start.3 = (bf16[256,768]{1,0:T(8,128)(2,1)S(1)}, bf16[256,768]{1,0:T(8,128)(2,1)}, u32[]{:S(2)}) copy-start(bf16[256,768]{1,0:T(8,128)(2,1)} %get-tuple-element.6) | copy-start | bytes 1179652
  38.0 1.1 %copy-start.4 = (bf16[256,768]{1,0:T(8,128)(2,1)S(1)}, bf16[256,768]{1,0:T(8,128)(2,1)}, u32[]{:S(2)}) copy-start(bf16[256,768]{1,0:T(8,128)(2,1)} %get-tuple-element.7) | copy-start | bytes 1179652
  38.1 10.8 %collective-permute-start.9 = (f32[2,2,96,256]{3,2,1,0:T(8,128)S(1)}, f32[2,2,96,256]{3,2,1,0:T(8,128)S(1)}, u32[]{:S(2)}, u32[]{:S(2)}) collective-permute-start(f32[2,2,96,256]{3,2,1,0:T(8,128)S(1)} %dynamic-slice_bitcast_fusion), channel_id=1, source_target_pairs={{0,1},{1,0},{2,3},{3,2},{4,5},{5,4},{6,7},{7,6},{8,9},{9,8},{10,11... | collective-permute-start | bytes 1179656 | tf_op jit(solution)/shard_map/ppermute | solution.py:23
  47.2 6.4 %collective-permute-start.4 = (f32[2,96,256]{2,1,0:T(8,128)S(1)}, f32[2,96,256]{2,1,0:T(8,128)S(1)}, u32[]{:S(2)}, u32[]{:S(2)}) collective-permute-start(f32[2,96,256]{2,1,0:T(8,128)S(1)} %dynamic-slice_bitcast_fusion.3), channel_id=1, source_target_pairs={{0,1},{1,0},{2,3},{3,2},{4,5},{5,4},{6,7},{7,6},{8,9},{9,8},{10,11... | collective-permute-start | bytes 589832 | tf_op jit(solution)/shard_map/ppermute | solution.py:23
  49.0 5.7 %collective-permute-start.10 = (f32[2,96,256]{2,1,0:T(8,128)S(1)}, f32[2,96,256]{2,1,0:T(8,128)S(1)}, u32[]{:S(2)}, u32[]{:S(2)}) collective-permute-start(f32[2,96,256]{2,1,0:T(8,128)S(1)} %dynamic-slice_bitcast_fusion.2), channel_id=1, source_target_pairs={{0,8},{4,12},{8,0},{12,4},{1,9},{5,13},{9,1},{13,5},{2,10},{6,14},... | collective-permute-start | bytes 589832 | tf_op jit(solution)/shard_map/ppermute | solution.py:23
  53.6 8.6 %collective-permute-start.5 = (f32[96,256]{1,0:T(8,128)S(1)}, f32[96,256]{1,0:T(8,128)S(1)}, u32[]{:S(2)}, u32[]{:S(2)}) collective-permute-start(f32[96,256]{1,0:T(8,128)S(1)} %dynamic-slice_bitcast_fusion.5), channel_id=1, source_target_pairs={{0,2},{1,3},{2,0},{3,1},{4,6},{5,7},{6,4},{7,5},{8,10},{9,11},{10,... | collective-permute-start | bytes 294920 | tf_op jit(solution)/shard_map/ppermute | solution.py:23
  54.8 9.4 %collective-permute-start.11 = (f32[96,256]{1,0:T(8,128)S(1)}, f32[96,256]{1,0:T(8,128)S(1)}, u32[]{:S(2)}, u32[]{:S(2)}) collective-permute-start(f32[96,256]{1,0:T(8,128)S(1)} %dynamic-slice_bitcast_fusion.4), channel_id=1, source_target_pairs={{0,2},{1,3},{2,0},{3,1},{4,6},{5,7},{6,4},{7,5},{8,10},{9,11},{10,... | collective-permute-start | bytes 294920 | tf_op jit(solution)/shard_map/ppermute | solution.py:23
  62.2 4.8 %collective-permute-start.6 = (f32[1,96,256]{2,1,0:T(8,128)S(1)}, f32[1,96,256]{2,1,0:T(8,128)S(1)}, u32[]{:S(2)}, u32[]{:S(2)}) collective-permute-start(f32[1,96,256]{2,1,0:T(8,128)S(1)} %fusion.15), channel_id=1, source_target_pairs={{0,8},{4,12},{8,0},{12,4},{1,9},{5,13},{9,1},{13,5},{2,10},{6,14},... | collective-permute-start | bytes 294920 | tf_op jit(solution)/shard_map/ppermute | solution.py:23
  64.2 4.8 %collective-permute-start.12 = (f32[1,96,256]{2,1,0:T(8,128)S(1)}, f32[1,96,256]{2,1,0:T(8,128)S(1)}, u32[]{:S(2)}, u32[]{:S(2)}) collective-permute-start(f32[1,96,256]{2,1,0:T(8,128)S(1)} %fusion.14), channel_id=1, source_target_pairs={{0,8},{4,12},{8,0},{12,4},{1,9},{5,13},{9,1},{13,5},{2,10},{6,14},... | collective-permute-start | bytes 294920 | tf_op jit(solution)/shard_map/ppermute | solution.py:23
  67.0 2.1 %collective-permute-start.7 = (f32[2,96,256]{2,1,0:T(8,128)S(1)}, f32[2,96,256]{2,1,0:T(8,128)S(1)}, u32[]{:S(2)}, u32[]{:S(2)}) collective-permute-start(f32[2,96,256]{2,1,0:T(8,128)S(1)} %maximum_bitcast_fusion), channel_id=1, source_target_pairs={{0,4},{4,0},{8,12},{12,8},{1,5},{5,1},{9,13},{13,9},{2,6},{6,2},{1... | collective-permute-start | bytes 589832 | tf_op jit(solution)/shard_map/ppermute | solution.py:23
  69.1 1.5 %collective-permute-start.13 = (f32[2,96,256]{2,1,0:T(8,128)S(1)}, f32[2,96,256]{2,1,0:T(8,128)S(1)}, u32[]{:S(2)}, u32[]{:S(2)}) collective-permute-start(f32[2,96,256]{2,1,0:T(8,128)S(1)} %maximum_bitcast_fusion.1), channel_id=1, source_target_pairs={{0,4},{4,0},{8,12},{12,8},{1,5},{5,1},{9,13},{13,9},{2,6},{6,2},{1... | collective-permute-start | bytes 589832 | tf_op jit(solution)/shard_map/ppermute | solution.py:23

commit v5 on v4

--- a/solution.py
+++ b/solution.py
@@ -208,8 +208,10 @@
         schedule = first if kv_head % 2 == 0 else second
         weight_parts.append(head_weight_grad(hidden_cols, kv_part, schedule, labels, lead))
     rows = weight_parts[0].shape[0] * weight_parts[0].shape[1]
-    weight_parts = [w.reshape(rows, 2, HEAD_SIZE) for w in weight_parts]
-    weight_grad = jnp.stack(weight_parts, 2).reshape(rows, 2 * KEY_VALUE_HEADS * HEAD_SIZE)
+    weight_parts = [w.reshape(rows, 2 * HEAD_SIZE) for w in weight_parts]
+    weight_grad = jnp.concatenate(
+        [w[:, :HEAD_SIZE] for w in weight_parts] + [w[:, HEAD_SIZE:] for w in weight_parts], 1
+    )
     return (jnp.concatenate(query_parts, 1), weight_grad)
 
 

time: 73.6 us -> 72 us (0.978)
  local copies, waits for them, and re-layouts: 5.76 us -> 3.5 us
    reshape x1 -> x0, local copies, waits for them, and re-layouts: 1.51 us -> none  [on_device(): jnp.stack(weight_parts, 2).reshape(rows, 2 * KEY_VALUE_HEADS * HEAD_SIZE)]
    concatenate x0 -> x1, other arithmetic: none -> 0.93 us  [on_device(): jnp.concatenate([w[:, :HEAD_SIZE] for w in weight_parts] + [w[:, HEAD_SIZ...]
    another operation x2 -> x0, local copies, waits for them, and re-layouts: 0.79 us -> none  [on_device(): jnp.stack(weight_parts, 2).reshape(rows, 2 * KEY_VALUE_HEADS * HEAD_SIZE)]
where the time goes in v5:
time: 72 us; the launch traced here: 71.6 us
  waiting for transfers between devices  25.1 us (35%)
  starting transfers between devices  20.1 us (28%)
  Pallas kernels  12.5 us (17%)
  other arithmetic  7.09 us (10%)
  local copies, waits for them, and re-layouts  3.5 us (5%)
  matrix products  2.27 us (3%)
  between operations  1.11 us (2%)
    ppermute x12, waiting for transfers between devices, exchange(): return lax.ppermute(block, axis, [(i, i ^ bit) for i in range(count)])  24.3 us
    pallas_call x2, Pallas kernels, window_grads(): pl.pallas_call(functools.partial(attention_kernel, kv_heads), grid=(1,),...  12.5 us
    ppermute x12, starting transfers between devices, exchange(): return lax.ppermute(block, axis, [(i, i ^ bit) for i in range(count)])  11.6 us
    ppermute x2, starting transfers between devices, shifted(): return lax.ppermute(block, axis, route)  8.46 us
    unnamed x13, local copies, waits for them, and re-layouts  2.29 us
    dot_general x4, matrix products, weight_rows(): jnp.einsum('td,tc->dc', hidden_cols, kv_parts, preferred_element_type=jnp...  2.27 us
  transfers between devices with their start and end apart: 14, of which 10 were waited for; matrix products, arithmetic and copies ran while one was open for 13% of the time, Pallas kernels for 17%

profile of v5, /device:TPU:0, one launch (start us, length us, event | category | flops | bytes accessed | tf_op | source)
XLA Modules:
  0.0 71.6 jit_solution(3807061686252388021)
XLA Ops:
  0.6 1.0 %pad_maximum_fusion.11 = bf16[256,512]{1,0:T(8,128)(2,1)S(1)} fusion(bf16[256,256]{1,0:T(8,128)(2,1)} %param.9, bf16[256,256]{1,0:T(8,128)(2,1)} %param.8), kind=kLoop, calls=%fused_computation.31 | loop fusion | flops 524288 | bytes 524288 | tf_op jit(solution)/shard_map/concatenate | solution.py:188
  1.7 4.9 %collective-permute-start = (bf16[256,512]{1,0:T(8,128)(2,1)S(1)}, bf16[256,512]{1,0:T(8,128)(2,1)S(1)}, u32[]{:S(2)}, u32[]{:S(2)}) collective-permute-start(bf16[256,512]{1,0:T(8,128)(2,1)S(1)} %pad_maximum_fusion.11), channel_id=1, source_target_pairs={{0,1},{1,2},{2,3},{3,4},{4,5},{5,6},{6,7},{7,8},{8,9},{9,10},{10,1... | collective-permute-start | bytes 786440 | tf_op jit(solution)/shard_map/ppermute | solution.py:18
  6.6 1.4 %copy.12 = bf16[256,1536]{0,1:T(8,128)(2,1)S(1)} copy(bf16[256,1536]{1,0:T(8,128)(2,1)} %param.6) | data formatting | bytes 1572864 | tf_op args[0]
  8.0 3.5 %collective-permute-start.1 = (bf16[256,1536]{0,1:T(8,128)(2,1)S(1)}, bf16[256,1536]{0,1:T(8,128)(2,1)S(1)}, u32[]{:S(2)}, u32[]{:S(2)}) collective-permute-start(bf16[256,1536]{0,1:T(8,128)(2,1)S(1)} %copy.12), channel_id=1, source_target_pairs={{0,1},{1,2},{2,3},{3,4},{4,5},{5,6},{6,7},{7,8},{8,9},{9,10},{10,1... | collective-permute-start | bytes 2359304 | tf_op jit(solution)/shard_map/ppermute | solution.py:18
  12.5 0.9 %copy.10.ks_ref = s32[512,1]{1,0:T(8,128)} copy(s32[512,1]{0,1:T(1,128)S(1)} %bitcast.99) | data formatting | bytes 4096 | tf_op jit(solution)/shard_map/reshape | solution.py:181
  14.3 6.2 %shard_map.77 = (bf16[256,768]{1,0:T(8,128)(2,1)}, f32[512,256]{1,0:T(8,128)}) custom-call(bf16[256,1536]{1,0:T(8,128)(2,1)} %q_ref.3, bf16[256,1536]{1,0:T(8,128)(2,1)} %g_ref.3, bf16[512,256]{1,0:T(8,128)(2,1)} %get-tuple-element.30.k_ref, bf16[512,256]{1,0:T(8,128)(2,1)} %get-tuple-element.31.v_ref, s32[1,256]{1,0:T(1,128)} %bitcast.100, ...), custom_call_target="tpu_custom_call" | custom-call | flops 1006632960 | bytes 2097152 | tf_op jit(solution)/shard_map/pallas_call | solution.py:164
  20.5 6.3 %shard_map.78 = (bf16[256,768]{1,0:T(8,128)(2,1)}, f32[512,256]{1,0:T(8,128)}) custom-call(bf16[256,1536]{1,0:T(8,128)(2,1)} %q_ref.3, bf16[256,1536]{1,0:T(8,128)(2,1)} %g_ref.3, bf16[512,256]{1,0:T(8,128)(2,1)} %get-tuple-element.30.k_ref, bf16[512,256]{1,0:T(8,128)(2,1)} %get-tuple-element.31.v_ref, s32[1,256]{1,0:T(1,128)} %bitcast.101, ...), custom_call_target="tpu_custom_call" | custom-call | flops 1006632960 | bytes 2097152 | tf_op jit(solution)/shard_map/pallas_call | solution.py:164
  26.9 1.3 %fusion.25 = (bf16[512,256]{1,0:T(8,128)(2,1)S(1)}, bf16[512,256]{1,0:T(8,128)(2,1)S(1)}) fusion(f32[512,256]{1,0:T(8,128)} %get-tuple-element.9), kind=kLoop, calls=%fused_computation.65 | loop fusion | flops 524288 | bytes 1048576 | tf_op jit(solution)/shard_map/convert_element_type | solution.py:65
  29.9 3.0 %collective-permute-start.2 = (f32[2,2,2,96,256]{4,3,2,1,0:T(8,128)S(1)}, f32[2,2,2,96,256]{4,3,2,1,0:T(8,128)S(1)}, u32[]{:S(2)}, u32[]{:S(2)}) collective-permute-start(f32[2,2,2,96,256]{4,3,2,1,0:T(8,128)S(1)} %bitcast.98), channel_id=1, source_target_pairs={{0,4},{4,0},{8,12},{12,8},{1,5},{5,1},{9,13},{13,9},{2,6},{6,2},{1... | collective-permute-start | bytes 2359304 | tf_op jit(solution)/shard_map/ppermute | solution.py:23
  35.1 2.7 %collective-permute-start.3 = (f32[2,2,96,256]{3,2,1,0:T(8,128)S(1)}, f32[2,2,96,256]{3,2,1,0:T(8,128)S(1)}, u32[]{:S(2)}, u32[]{:S(2)}) collective-permute-start(f32[2,2,96,256]{3,2,1,0:T(8,128)S(1)} %dynamic-slice_bitcast_fusion.1), channel_id=1, source_target_pairs={{0,8},{4,12},{8,0},{12,4},{1,9},{5,13},{9,1},{13,5},{2,10},{6,14},... | collective-permute-start | bytes 1179656 | tf_op jit(solution)/shard_map/ppermute | solution.py:23
  39.1 0.9 %pad_maximum_fusion.1 = bf16[256,1536]{1,0:T(8,128)(2,1)} fusion(bf16[256,768]{1,0:T(8,128)(2,1)S(1)} %copy-done.4, bf16[256,768]{1,0:T(8,128)(2,1)S(1)} %copy-done.3), kind=kLoop, calls=%fused_computation.5 | loop fusion | flops 1572864 | bytes 1572864 | tf_op jit(solution)/shard_map/concatenate | solution.py:215
  40.0 7.1 %collective-permute-done.3 = f32[2,2,96,256]{3,2,1,0:T(8,128)S(1)} collective-permute-done((f32[2,2,96,256]{3,2,1,0:T(8,128)S(1)}, f32[2,2,96,256]{3,2,1,0:T(8,128)S(1)}, u32[]{:S(2)}, u32[]{:S(2)}) %collective-permute-start.3) | collective-permute-done | bytes 393248 | tf_op jit(solution)/shard_map/ppermute | solution.py:23
  47.3 1.6 %collective-permute-done.9 = f32[2,2,96,256]{3,2,1,0:T(8,128)S(1)} collective-permute-done((f32[2,2,96,256]{3,2,1,0:T(8,128)S(1)}, f32[2,2,96,256]{3,2,1,0:T(8,128)S(1)}, u32[]{:S(2)}, u32[]{:S(2)}) %collective-permute-start.9) | collective-permute-done | bytes 393248 | tf_op jit(solution)/shard_map/ppermute | solution.py:23
  49.0 1.0 %collective-permute-start.10 = (f32[2,96,256]{2,1,0:T(8,128)S(1)}, f32[2,96,256]{2,1,0:T(8,128)S(1)}, u32[]{:S(2)}, u32[]{:S(2)}) collective-permute-start(f32[2,96,256]{2,1,0:T(8,128)S(1)} %dynamic-slice_bitcast_fusion.2), channel_id=1, source_target_pairs={{0,8},{4,12},{8,0},{12,4},{1,9},{5,13},{9,1},{13,5},{2,10},{6,14},... | collective-permute-start | bytes 589832 | tf_op jit(solution)/shard_map/ppermute | solution.py:23
  50.0 3.6 %collective-permute-done.4 = f32[2,96,256]{2,1,0:T(8,128)S(1)} collective-permute-done((f32[2,96,256]{2,1,0:T(8,128)S(1)}, f32[2,96,256]{2,1,0:T(8,128)S(1)}, u32[]{:S(2)}, u32[]{:S(2)}) %collective-permute-start.4) | collective-permute-done | bytes 196640 | tf_op jit(solution)/shard_map/ppermute | solution.py:23
  53.7 1.1 %collective-permute-done.10 = f32[2,96,256]{2,1,0:T(8,128)S(1)} collective-permute-done((f32[2,96,256]{2,1,0:T(8,128)S(1)}, f32[2,96,256]{2,1,0:T(8,128)S(1)}, u32[]{:S(2)}, u32[]{:S(2)}) %collective-permute-start.10) | collective-permute-done | bytes 196640 | tf_op jit(solution)/shard_map/ppermute | solution.py:23
  54.8 1.9 %collective-permute-start.11 = (f32[96,256]{1,0:T(8,128)S(1)}, f32[96,256]{1,0:T(8,128)S(1)}, u32[]{:S(2)}, u32[]{:S(2)}) collective-permute-start(f32[96,256]{1,0:T(8,128)S(1)} %dynamic-slice_bitcast_fusion.4), channel_id=1, source_target_pairs={{0,2},{1,3},{2,0},{3,1},{4,6},{5,7},{6,4},{7,5},{8,10},{9,11},{10,... | collective-permute-start | bytes 294920 | tf_op jit(solution)/shard_map/ppermute | solution.py:23
  56.8 5.5 %collective-permute-done.5 = f32[96,256]{1,0:T(8,128)S(1)} collective-permute-done((f32[96,256]{1,0:T(8,128)S(1)}, f32[96,256]{1,0:T(8,128)S(1)}, u32[]{:S(2)}, u32[]{:S(2)}) %collective-permute-start.5) | collective-permute-done | bytes 98336 | tf_op jit(solution)/shard_map/ppermute | solution.py:23
  62.2 1.4 %collective-permute-start.6 = (f32[1,96,256]{2,1,0:T(8,128)S(1)}, f32[1,96,256]{2,1,0:T(8,128)S(1)}, u32[]{:S(2)}, u32[]{:S(2)}) collective-permute-start(f32[1,96,256]{2,1,0:T(8,128)S(1)} %fusion.15), channel_id=1, source_target_pairs={{0,8},{4,12},{8,0},{12,4},{1,9},{5,13},{9,1},{13,5},{2,10},{6,14},... | collective-permute-start | bytes 294920 | tf_op jit(solution)/shard_map/ppermute | solution.py:23
  64.2 1.2 %collective-permute-start.12 = (f32[1,96,256]{2,1,0:T(8,128)S(1)}, f32[1,96,256]{2,1,0:T(8,128)S(1)}, u32[]{:S(2)}, u32[]{:S(2)}) collective-permute-start(f32[1,96,256]{2,1,0:T(8,128)S(1)} %fusion.14), channel_id=1, source_target_pairs={{0,8},{4,12},{8,0},{12,4},{1,9},{5,13},{9,1},{13,5},{2,10},{6,14},... | collective-permute-start | bytes 294920 | tf_op jit(solution)/shard_map/ppermute | solution.py:23
  65.4 1.6 %collective-permute-done.6 = f32[1,96,256]{2,1,0:T(8,128)S(1)} collective-permute-done((f32[1,96,256]{2,1,0:T(8,128)S(1)}, f32[1,96,256]{2,1,0:T(8,128)S(1)}, u32[]{:S(2)}, u32[]{:S(2)}) %collective-permute-start.6) | collective-permute-done | bytes 98336 | tf_op jit(solution)/shard_map/ppermute | solution.py:23
  67.1 1.9 %collective-permute-done.12 = f32[1,96,256]{2,1,0:T(8,128)S(1)} collective-permute-done((f32[1,96,256]{2,1,0:T(8,128)S(1)}, f32[1,96,256]{2,1,0:T(8,128)S(1)}, u32[]{:S(2)}, u32[]{:S(2)}) %collective-permute-start.12) | collective-permute-done | bytes 98336 | tf_op jit(solution)/shard_map/ppermute | solution.py:23
  69.3 1.3 %collective-permute-done.13 = f32[2,96,256]{2,1,0:T(8,128)S(1)} collective-permute-done((f32[2,96,256]{2,1,0:T(8,128)S(1)}, f32[2,96,256]{2,1,0:T(8,128)S(1)}, u32[]{:S(2)}, u32[]{:S(2)}) %collective-permute-start.13) | collective-permute-done | bytes 196640 | tf_op jit(solution)/shard_map/ppermute | solution.py:23
  70.7 0.9 %pad_maximum_fusion.2 = f32[384,512]{1,0:T(8,128)} fusion(f32[384,128]{1,0:T(8,128)S(1)} %get-tuple-element.17, f32[384,128]{1,0:T(8,128)S(1)} %get-tuple-element.15, f32[384,128]{1,0:T(8,128)S(1)} %get-tuple-element.16, f32[384,128]{1,0:T(8,128)S(1)} %get-tuple-element.14), kind=kLoop, calls=%fused_computation.6 | loop fusion | flops 589824 | bytes 1572864 | tf_op jit(solution)/shard_map/concatenate | solution.py:212
  (64 shorter events, 8.2 us)
Async XLA Ops:
  0.6 12.8 %copy-start.1 = (bf16[256,256]{1,0:T(8,128)(2,1)S(1)}, bf16[256,256]{1,0:T(8,128)(2,1)}, u32[]{:S(2)}) copy-start(bf16[256,256]{1,0:T(8,128)(2,1)} %param.8) | copy-start | bytes 393220
  0.6 12.8 %copy-start.2 = (bf16[256,256]{1,0:T(8,128)(2,1)S(1)}, bf16[256,256]{1,0:T(8,128)(2,1)}, u32[]{:S(2)}) copy-start(bf16[256,256]{1,0:T(8,128)(2,1)} %param.9) | copy-start | bytes 393220
  1.7 11.7 %collective-permute-start = (bf16[256,512]{1,0:T(8,128)(2,1)S(1)}, bf16[256,512]{1,0:T(8,128)(2,1)S(1)}, u32[]{:S(2)}, u32[]{:S(2)}) collective-permute-start(bf16[256,512]{1,0:T(8,128)(2,1)S(1)} %pad_maximum_fusion.11), channel_id=1, source_target_pairs={{0,1},{1,2},{2,3},{3,4},{4,5},{5,6},{6,7},{7,8},{8,9},{9,10},{10,1... | collective-permute-start | bytes 786440 | tf_op jit(solution)/shard_map/ppermute | solution.py:18
  8.0 21.0 %collective-permute-start.1 = (bf16[256,1536]{0,1:T(8,128)(2,1)S(1)}, bf16[256,1536]{0,1:T(8,128)(2,1)S(1)}, u32[]{:S(2)}, u32[]{:S(2)}) collective-permute-start(bf16[256,1536]{0,1:T(8,128)(2,1)S(1)} %copy.12), channel_id=1, source_target_pairs={{0,1},{1,2},{2,3},{3,4},{4,5},{5,6},{6,7},{7,8},{8,9},{9,10},{10,1... | collective-permute-start | bytes 2359304 | tf_op jit(solution)/shard_map/ppermute | solution.py:18
  12.5 1.8 %copy-start.5 = (s32[256]{0:T(256)}, s32[256]{0:T(256)S(1)}, u32[]{:S(2)}) copy-start(s32[256]{0:T(256)S(1)} %get-tuple-element.29) | copy-start | bytes 3076
  20.5 6.3 %copy-start = (f32[512,256]{1,0:T(8,128)S(1)}, f32[512,256]{1,0:T(8,128)}, u32[]{:S(2)}) copy-start(f32[512,256]{1,0:T(8,128)} %get-tuple-element.8) | copy-start | bytes 1572868
  29.9 5.0 %collective-permute-start.2 = (f32[2,2,2,96,256]{4,3,2,1,0:T(8,128)S(1)}, f32[2,2,2,96,256]{4,3,2,1,0:T(8,128)S(1)}, u32[]{:S(2)}, u32[]{:S(2)}) collective-permute-start(f32[2,2,2,96,256]{4,3,2,1,0:T(8,128)S(1)} %bitcast.98), channel_id=1, source_target_pairs={{0,4},{4,0},{8,12},{12,8},{1,5},{5,1},{9,13},{13,9},{2,6},{6,2},{1... | collective-permute-start | bytes 2359304 | tf_op jit(solution)/shard_map/ppermute | solution.py:23
  33.6 4.3 %collective-permute-start.8 = (f32[2,2,2,96,256]{4,3,2,1,0:T(8,128)S(1)}, f32[2,2,2,96,256]{4,3,2,1,0:T(8,128)S(1)}, u32[]{:S(2)}, u32[]{:S(2)}) collective-permute-start(f32[2,2,2,96,256]{4,3,2,1,0:T(8,128)S(1)} %bitcast.97), channel_id=1, source_target_pairs={{0,4},{4,0},{8,12},{12,8},{1,5},{5,1},{9,13},{13,9},{2,6},{6,2},{1... | collective-permute-start | bytes 2359304 | tf_op jit(solution)/shard_map/ppermute | solution.py:23
  35.1 12.0 %collective-permute-start.3 = (f32[2,2,96,256]{3,2,1,0:T(8,128)S(1)}, f32[2,2,96,256]{3,2,1,0:T(8,128)S(1)}, u32[]{:S(2)}, u32[]{:S(2)}) collective-permute-start(f32[2,2,96,256]{3,2,1,0:T(8,128)S(1)} %dynamic-slice_bitcast_fusion.1), channel_id=1, source_target_pairs={{0,8},{4,12},{8,0},{12,4},{1,9},{5,13},{9,1},{13,5},{2,10},{6,14},... | collective-permute-start | bytes 1179656 | tf_op jit(solution)/shard_map/ppermute | solution.py:23
  38.0 1.0 %copy-start.3 = (bf16[256,768]{1,0:T(8,128)(2,1)S(1)}, bf16[256,768]{1,0:T(8,128)(2,1)}, u32[]{:S(2)}) copy-start(bf16[256,768]{1,0:T(8,128)(2,1)} %get-tuple-element.6) | copy-start | bytes 1179652
  38.0 1.1 %copy-start.4 = (bf16[256,768]{1,0:T(8,128)(2,1)S(1)}, bf16[256,768]{1,0:T(8,128)(2,1)}, u32[]{:S(2)}) copy-start(bf16[256,768]{1,0:T(8,128)(2,1)} %get-tuple-element.7) | copy-start | bytes 1179652
  38.1 10.8 %collective-permute-start.9 = (f32[2,2,96,256]{3,2,1,0:T(8,128)S(1)}, f32[2,2,96,256]{3,2,1,0:T(8,128)S(1)}, u32[]{:S(2)}, u32[]{:S(2)}) collective-permute-start(f32[2,2,96,256]{3,2,1,0:T(8,128)S(1)} %dynamic-slice_bitcast_fusion), channel_id=1, source_target_pairs={{0,1},{1,0},{2,3},{3,2},{4,5},{5,4},{6,7},{7,6},{8,9},{9,8},{10,11... | collective-permute-start | bytes 1179656 | tf_op jit(solution)/shard_map/ppermute | solution.py:23
  47.2 6.4 %collective-permute-start.4 = (f32[2,96,256]{2,1,0:T(8,128)S(1)}, f32[2,96,256]{2,1,0:T(8,128)S(1)}, u32[]{:S(2)}, u32[]{:S(2)}) collective-permute-start(f32[2,96,256]{2,1,0:T(8,128)S(1)} %dynamic-slice_bitcast_fusion.3), channel_id=1, source_target_pairs={{0,1},{1,0},{2,3},{3,2},{4,5},{5,4},{6,7},{7,6},{8,9},{9,8},{10,11... | collective-permute-start | bytes 589832 | tf_op jit(solution)/shard_map/ppermute | solution.py:23
  49.0 5.7 %collective-permute-start.10 = (f32[2,96,256]{2,1,0:T(8,128)S(1)}, f32[2,96,256]{2,1,0:T(8,128)S(1)}, u32[]{:S(2)}, u32[]{:S(2)}) collective-permute-start(f32[2,96,256]{2,1,0:T(8,128)S(1)} %dynamic-slice_bitcast_fusion.2), channel_id=1, source_target_pairs={{0,8},{4,12},{8,0},{12,4},{1,9},{5,13},{9,1},{13,5},{2,10},{6,14},... | collective-permute-start | bytes 589832 | tf_op jit(solution)/shard_map/ppermute | solution.py:23
  53.6 8.6 %collective-permute-start.5 = (f32[96,256]{1,0:T(8,128)S(1)}, f32[96,256]{1,0:T(8,128)S(1)}, u32[]{:S(2)}, u32[]{:S(2)}) collective-permute-start(f32[96,256]{1,0:T(8,128)S(1)} %dynamic-slice_bitcast_fusion.5), channel_id=1, source_target_pairs={{0,2},{1,3},{2,0},{3,1},{4,6},{5,7},{6,4},{7,5},{8,10},{9,11},{10,... | collective-permute-start | bytes 294920 | tf_op jit(solution)/shard_map/ppermute | solution.py:23
  54.8 9.4 %collective-permute-start.11 = (f32[96,256]{1,0:T(8,128)S(1)}, f32[96,256]{1,0:T(8,128)S(1)}, u32[]{:S(2)}, u32[]{:S(2)}) collective-permute-start(f32[96,256]{1,0:T(8,128)S(1)} %dynamic-slice_bitcast_fusion.4), channel_id=1, source_target_pairs={{0,2},{1,3},{2,0},{3,1},{4,6},{5,7},{6,4},{7,5},{8,10},{9,11},{10,... | collective-permute-start | bytes 294920 | tf_op jit(solution)/shard_map/ppermute | solution.py:23
  62.2 4.8 %collective-permute-start.6 = (f32[1,96,256]{2,1,0:T(8,128)S(1)}, f32[1,96,256]{2,1,0:T(8,128)S(1)}, u32[]{:S(2)}, u32[]{:S(2)}) collective-permute-start(f32[1,96,256]{2,1,0:T(8,128)S(1)} %fusion.15), channel_id=1, source_target_pairs={{0,8},{4,12},{8,0},{12,4},{1,9},{5,13},{9,1},{13,5},{2,10},{6,14},... | collective-permute-start | bytes 294920 | tf_op jit(solution)/shard_map/ppermute | solution.py:23
  64.2 4.8 %collective-permute-start.12 = (f32[1,96,256]{2,1,0:T(8,128)S(1)}, f32[1,96,256]{2,1,0:T(8,128)S(1)}, u32[]{:S(2)}, u32[]{:S(2)}) collective-permute-start(f32[1,96,256]{2,1,0:T(8,128)S(1)} %fusion.14), channel_id=1, source_target_pairs={{0,8},{4,12},{8,0},{12,4},{1,9},{5,13},{9,1},{13,5},{2,10},{6,14},... | collective-permute-start | bytes 294920 | tf_op jit(solution)/shard_map/ppermute | solution.py:23
  67.0 2.1 %collective-permute-start.7 = (f32[2,96,256]{2,1,0:T(8,128)S(1)}, f32[2,96,256]{2,1,0:T(8,128)S(1)}, u32[]{:S(2)}, u32[]{:S(2)}) collective-permute-start(f32[2,96,256]{2,1,0:T(8,128)S(1)} %maximum_bitcast_fusion), channel_id=1, source_target_pairs={{0,4},{4,0},{8,12},{12,8},{1,5},{5,1},{9,13},{13,9},{2,6},{6,2},{1... | collective-permute-start | bytes 589832 | tf_op jit(solution)/shard_map/ppermute | solution.py:23
  69.1 1.5 %collective-permute-start.13 = (f32[2,96,256]{2,1,0:T(8,128)S(1)}, f32[2,96,256]{2,1,0:T(8,128)S(1)}, u32[]{:S(2)}, u32[]{:S(2)}) collective-permute-start(f32[2,96,256]{2,1,0:T(8,128)S(1)} %maximum_bitcast_fusion.1), channel_id=1, source_target_pairs={{0,4},{4,0},{8,12},{12,8},{1,5},{5,1},{9,13},{13,9},{2,6},{6,2},{1... | collective-permute-start | bytes 589832 | tf_op jit(solution)/shard_map/ppermute | solution.py:23
